TPU v7x, 32 devices: a whole 2x2x4 slice. The times are simulated.
32 devices in a mesh: groups: 2 (over y), chan: 4 (over z), tm: 4 (over x, core).
Axes of the slice: x: 2, y: 2, z: 4, core: 2. Of those that a mesh axis runs over, the one named last changes fastest.
Arguments:
- samples: bfloat16 [2, 16, 1024, 4096], P(None, None, ('groups', 'chan'), 'tm'), parts along dimension 2, may hold values from -6 to 6
- station_gain: float32 [1024], P(('groups', 'chan')), parts along dimension 0, may hold values from 0.5 to 4
- station_map: int32 [1024], P('groups'), parts along dimension 0, may hold values from 0 to 511, each once
- steer_phase: float32 [16, 512, 1024], P('chan', None, ('groups', 'tm')), parts along dimension 2, may hold values from -3.140625 to 3.140625
Outputs:
- beams_out: bfloat16 [16, 4096, 2, 1024], P('chan', 'tm', None, 'groups'), parts along dimension 3
There are 2 independent parts, one for each index of `groups`. A program takes and returns all parts, laid end to end along the dimension named above; each array names one. Nothing has to cross between parts.
Inputs may be any that keep to these rules, and one draw needn't show every extreme that they name: station_map names each of the 512 stations once.
All inputs are finite; a program needn't handle non-finite values.
Results may differ from a plain program's by a relative error of at most 0.015.
Values may be sent and summed in bfloat16 or wider, within the bound.
No kernel may reach another device: no remote copies, remote signals or barrier semaphores. Data moves between devices by JAX's collectives and lax.ppermute only.
A program may use at most 256 MiB of HBM per device.

v0:
```python
import math

import jax
import jax.numpy as jnp
from jax import lax
from jax.sharding import PartitionSpec as P

ITERS = 8


def dft_table(count):
    index = jnp.arange(count, dtype=jnp.int32)
    turns = (index[:, None] * index[None, :] % count).astype(jnp.float32)
    angle_grid = 2.0 * math.pi * turns / count
    cosine = jnp.cos(angle_grid)
    sine = jnp.sin(angle_grid)
    upper = jnp.concatenate((cosine, sine), axis=1)
    lower = jnp.concatenate((-sine, cosine), axis=1)
    return jnp.concatenate((upper, lower), axis=0).astype(jnp.bfloat16)


def gram_blocks(stacked):
    return jnp.einsum("cat,cbt->cab", stacked, stacked, preferred_element_type=jnp.float32)


def local(samples, station_gain, station_map, steer_phase):
    high = lax.Precision.HIGHEST
    count = samples.shape[1]
    row_count = samples.shape[2]
    spec_count = samples.shape[3]
    channelized = jnp.dot(
        dft_table(count), samples.reshape(2 * count, -1), preferred_element_type=jnp.float32
    )
    channelized = channelized.reshape(2, count, row_count, spec_count)
    spectra = (channelized * station_gain[None, None, :, None]).astype(jnp.bfloat16)
    owned = lax.all_to_all(spectra, "chan", split_axis=1, concat_axis=2, tiled=True)
    stations = owned.shape[2]
    stacked = jnp.concatenate((owned[0], owned[1]), axis=1)
    spectra_total = spec_count * lax.axis_size("tm")
    gram_sum = gram_blocks(stacked)
    part_real = gram_sum[:, :stations, :stations] + gram_sum[:, stations:, stations:]
    part_imag = gram_sum[:, stations:, :stations] - gram_sum[:, :stations, stations:]
    cov_real, cov_imag = (
        lax.psum(part_real.astype(jnp.bfloat16), "tm").astype(jnp.float32),
        lax.psum(part_imag.astype(jnp.bfloat16), "tm").astype(jnp.float32),
    )
    cov_real = cov_real / spectra_total
    cov_imag = cov_imag / spectra_total
    loading = jnp.sum(jnp.diagonal(cov_real, axis1=1, axis2=2), axis=1) / stations
    row_mass = jnp.sum(jnp.sqrt(cov_real * cov_real + cov_imag * cov_imag), axis=2)
    bound = loading + jnp.max(row_mass, axis=1)
    center = ((bound + loading) / 2.0)[:, None, None]
    radius = ((bound - loading) / 2.0)[:, None, None]
    loading = loading[:, None, None]
    phase_rows = jnp.take(steer_phase, station_map, axis=1)
    steer_real = jnp.cos(phase_rows)
    steer_imag = jnp.sin(phase_rows)
    sol_real = jnp.zeros_like(steer_real)
    sol_imag = jnp.zeros_like(steer_imag)
    res_real, res_imag = (steer_real, steer_imag)
    dir_real = res_real / center
    dir_imag = res_imag / center
    rho_prev = radius / center
    for iteration in range(ITERS):
        sol_real = sol_real + dir_real
        sol_imag = sol_imag + dir_imag
        out_real = jnp.einsum("cjk,ckb->cjb", cov_real, dir_real, precision=high) - jnp.einsum(
            "cjk,ckb->cjb", cov_imag, dir_imag, precision=high
        )
        out_imag = jnp.einsum("cjk,ckb->cjb", cov_imag, dir_real, precision=high) + jnp.einsum(
            "cjk,ckb->cjb", cov_real, dir_imag, precision=high
        )
        img_real = out_real + loading * dir_real
        img_imag = out_imag + loading * dir_imag
        res_real = res_real - img_real
        res_imag = res_imag - img_imag
        rho_next = 1.0 / (2.0 * center / radius - rho_prev)
        dir_real = rho_next * rho_prev * dir_real + 2.0 * rho_next / radius * res_real
        dir_imag = rho_next * rho_prev * dir_imag + 2.0 * rho_next / radius * res_imag
        rho_prev = rho_next
    response = jnp.sum(steer_real * sol_real + steer_imag * sol_imag, axis=1, keepdims=True)
    weights = jnp.stack(
        ((sol_real / response).astype(jnp.bfloat16), (sol_imag / response).astype(jnp.bfloat16)),
        axis=1,
    )
    block_part = lax.all_gather(weights, "tm", axis=3, tiled=True)
    weight_real = block_part[:, 0]
    weight_imag = block_part[:, 1]
    weight_cat = jnp.stack(
        (
            jnp.concatenate((weight_real, weight_imag), axis=1),
            jnp.concatenate((-weight_imag, weight_real), axis=1),
        ),
        axis=2,
    )
    formed = jnp.einsum("cat,cakb->ctkb", stacked, weight_cat, preferred_element_type=jnp.float32)
    return formed.astype(jnp.bfloat16)


def solution(mesh):
    in_specs = (
        P(None, None, ("groups", "chan"), "tm"),
        P(("groups", "chan")),
        P("groups"),
        P("chan", None, ("groups", "tm")),
    )
    out_specs = P("chan", "tm", None, "groups")
    return jax.shard_map(local, mesh=mesh, in_specs=in_specs, out_specs=out_specs, check_vma=False)
```

profile of v0, /device:TPU:0, one launch (start us, length us, event | category | flops | bytes accessed | tf_op | source)
XLA Modules:
  0.0 677.3 jit_solution(14381816873697495504)
XLA Ops:
  6.5 0.0 copy-start
  6.5 0.0 all-reduce.3.cloned.1.call-start
  6.5 0.1 negate_convert_fusion
  6.6 0.1 fusion.136
  6.7 0.1 maximum_maximum_fusion
  6.7 17.6 %multiply_convert_fusion = bf16[2,16,128,1024]{3,1,2,0:T(8,128)(2,1)} fusion(f32[128]{0:T(128)} %param.5, bf16[2,16,32,1]{2,1,3,0:T(8,128)(2,1)S(1)} %bitcast.120, bf16[4,8,128,1024]{3,2,1,0:T(8,128)(2,1)} %bitcast.121), kind=kOutput, calls=%fused_computation.2 | convolution fusion | flops 276824064 | bytes 16779776 | tf_op jit(solution)/shard_map/dot_general | solution.py:31
  24.4 11.3 %copy.26 = bf16[2,16,128,1024]{3,2,0,1:T(8,128)(2,1)} copy(bf16[2,16,128,1024]{3,1,2,0:T(8,128)(2,1)} %multiply_convert_fusion) | data formatting | bytes 16777216 | tf_op jit(solution)/shard_map/convert_element_type | solution.py:35
  35.7 192.4 %all_to_all.15 = bf16[2,16,128,1024]{3,2,0,1:T(8,128)(2,1)} all-to-all(bf16[2,16,128,1024]{3,2,0,1:T(8,128)(2,1)} %copy.26), channel_id=1, replica_groups=mesh['groups'=2,'chan'=4,'tm'=4] {'chan'}, dimensions={1} | all-to-all | bytes 16777216 | tf_op jit(solution)/shard_map/all_to_all | solution.py:36
  228.1 8.4 %copy.52 = bf16[2,4,4,128,1024]{4,3,1,2,0:T(8,128)(2,1)} copy(bf16[2,4,4,128,1024]{4,3,0,2,1:T(8,128)(2,1)} %bitcast.115) | data formatting | bytes 16777216 | tf_op jit(solution)/shard_map/all_to_all | solution.py:36
  236.4 6.1 fusion.172
  242.5 17.7 %fusion.10 = f32[4,1024,1024]{2,1,0:T(8,128)} fusion(bf16[4,512,1024]{2,1,0:T(8,128)(2,1)} %bitcast.118, bf16[4,512,1024]{2,1,0:T(8,128)(2,1)} %bitcast.116), kind=kOutput, calls=%fused_computation.13 | convolution fusion | flops 8606711808 | bytes 25165824 | tf_op jit(solution)/shard_map/cat,cbt->cab/dot_general | solution.py:23
  260.1 8.8 %fusion.12 = (bf16[4,512,512]{2,1,0:T(8,128)(2,1)}, bf16[4,512,512]{2,1,0:T(8,128)(2,1)}) fusion(f32[4,1024,1024]{2,1,0:T(8,128)} %fusion.10), kind=kLoop, calls=%fused_computation.17 | loop fusion | flops 4194304 | bytes 20971520 | tf_op jit(solution)/shard_map/convert_element_type | solution.py:44
  268.9 0.0 all-reduce.3.cloned.1.call-update
  269.0 0.0 all-gather.2.cloned.1.call-start
  269.0 0.6 copy-done.6
  269.6 0.0 copy-done
  269.6 3.4 gather_fusion
  273.0 80.9 %all-reduce.3.cloned.1.call-done = (bf16[4,512,512]{2,1,0:T(8,128)(2,1)}, bf16[4,512,512]{2,1,0:T(8,128)(2,1)}) async-done(((bf16[4,512,512]{2,1,0:T(8,128)(2,1)}, bf16[4,512,512]{2,1,0:T(8,128)(2,1)}), (bf16[4,512,512]{2,1,0:T(8,128)(2,1)}, bf16[4,512,512]{2,1,0:T(8,128)(2,1)})) %all-reduce.3.cloned.1.call-update) | async-done | bytes 4194320 | tf_op jit(solution)/shard_map/psum | solution.py:45
  353.9 6.3 convert_multiply_fusion.15
  360.2 60.3 %copy.28 = f32[4,512,512]{0,2,1:T(8,128)} copy(f32[4,512,512]{2,1,0:T(8,128)} %get-tuple-element.27) | data formatting | bytes 8388608 | tf_op jit(solution)/shard_map/div | solution.py:47
  420.5 5.7 gather_fusion.1
  426.2 0.1 reduce_sum.27
  426.3 0.1 reduce_max.9
  426.5 0.0 copy-done.2
  426.5 8.6 %fusion.26 = f32[4,512,128]{2,1,0:T(8,128)S(1)} fusion(bf16[4,512,512]{2,1,0:T(8,128)(2,1)S(1)} %copy-done.2, f32[512,4,128]{2,0,1:T(8,128)} %gather_fusion, f32[4]{0:T(128)S(1)} %get-tuple-element.16, pred[512]{0:T(512)(128)(4,1)S(1)} %compare_and_fusion), kind=kOutput, calls=%fused_computation.35 | convolution fusion | flops 1613234176 | bytes 4194832 | tf_op jit(solution)/shard_map/cjk,ckb->cjb/dot_general | solution.py:67
  435.2 9.1 %fusion.25 = f32[4,512,128]{2,1,0:T(8,128)S(1)} fusion(bf16[4,512,512]{2,1,0:T(8,128)(2,1)S(1)} %copy-done.2, f32[512,4,128]{2,0,1:T(8,128)} %gather_fusion, f32[4]{0:T(128)S(1)} %get-tuple-element.16, pred[512]{0:T(512)(128)(4,1)S(1)} %compare_and_fusion), kind=kOutput, calls=%fused_computation.34 | convolution fusion | flops 1613234176 | bytes 4194832 | tf_op jit(solution)/shard_map/cjk,ckb->cjb/dot_general | solution.py:70
  444.3 0.0 copy-done.3
  444.3 0.0 copy-done.5
  444.3 10.7 %fusion.112 = f32[4,512,128]{2,1,0:T(8,128)S(1)} fusion(f32[4,512,128]{2,1,0:T(8,128)S(1)} %fusion.26, bf16[4,512,512]{2,1,0:T(8,128)(2,1)S(1)} %copy-done.3, f32[512,4,128]{2,0,1:T(8,128)S(1)} %copy-done.5, f32[4]{0:T(128)S(1)} %get-tuple-element.48, pred[512]{0:T(512)(128)(4,1)S(1)} %compare_and_fusion, f32[4]{0:T(128)S(1)} %get-tuple-element.16), kind=kOutput, calls=%fused_computation.124 | convolution fusion | flops 1614807040 | bytes 5243424 | tf_op jit(solution)/shard_map/cjk,ckb->cjb/dot_general | solution.py:67
  455.1 10.8 %fusion.108 = f32[4,512,128]{2,1,0:T(8,128)S(1)} fusion(f32[4,512,128]{2,1,0:T(8,128)S(1)} %fusion.25, bf16[4,512,512]{2,1,0:T(8,128)(2,1)S(1)} %copy-done.3, f32[512,4,128]{2,0,1:T(8,128)S(1)} %copy-done.5, f32[4]{0:T(128)S(1)} %get-tuple-element.48, pred[512]{0:T(512)(128)(4,1)S(1)} %compare_and_fusion, f32[4]{0:T(128)S(1)} %get-tuple-element.16), kind=kOutput, calls=%fused_computation.120 | convolution fusion | flops 1614807040 | bytes 5243424 | tf_op jit(solution)/shard_map/cjk,ckb->cjb/dot_general | solution.py:70
  465.9 7.5 %fusion.23 = f32[4,512,128]{2,1,0:T(8,128)S(1)} fusion(bf16[4,512,512]{2,1,0:T(8,128)(2,1)S(1)} %copy-done.2, f32[4,512,128]{2,1,0:T(8,128)S(1)} %fusion.112, f32[4]{0:T(128)S(1)} %get-tuple-element.46, f32[4]{0:T(128)S(1)} %get-tuple-element.47, f32[512,4,128]{2,0,1:T(8,128)S(1)} %copy-done.5, f32[4]{0:T(128)S(1)} %get-tuple-element.16, ...), kind=kOutput, calls=%fused_computation.32 | convolution fusion | flops 1614020608 | bytes 5243440 | tf_op jit(solution)/shard_map/cjk,ckb->cjb/dot_general | solution.py:70
  473.4 7.9 %fusion.24 = f32[4,512,128]{2,1,0:T(8,128)S(1)} fusion(bf16[4,512,512]{2,1,0:T(8,128)(2,1)S(1)} %copy-done.2, f32[4,512,128]{2,1,0:T(8,128)S(1)} %fusion.108, f32[4]{0:T(128)S(1)} %get-tuple-element.46, f32[4]{0:T(128)S(1)} %get-tuple-element.47, f32[512,4,128]{2,0,1:T(8,128)S(1)} %copy-done.5, f32[4]{0:T(128)S(1)} %get-tuple-element.16, ...), kind=kOutput, calls=%fused_computation.33 | convolution fusion | flops 1614020608 | bytes 5243440 | tf_op jit(solution)/shard_map/cjk,ckb->cjb/dot_general | solution.py:67
  481.3 11.1 %fusion.110 = f32[4,512,128]{2,1,0:T(8,128)S(1)} fusion(f32[4,512,128]{2,1,0:T(8,128)S(1)} %fusion.112, f32[4,512,128]{2,1,0:T(8,128)S(1)} %fusion.24, bf16[4,512,512]{2,1,0:T(8,128)(2,1)S(1)} %copy-done.3, f32[4]{0:T(128)S(1)} %get-tuple-element.48, f32[4]{0:T(128)S(1)} %get-tuple-element.46, f32[4]{0:T(128)S(1)} %get-tuple-element.47, ...), kind=kOutput, calls=%fused_computation.122 | convolution fusion | flops 1616379904 | bytes 6292032 | tf_op jit(solution)/shard_map/cjk,ckb->cjb/dot_general | solution.py:67
  492.4 11.9 %multiply_add_fusion.10 = (f32[4,512,128]{2,1,0:T(8,128)S(1)}, f32[4,512,128]{2,1,0:T(8,128)S(1)}, f32[4,512,128]{2,1,0:T(8,128)S(1)}) fusion(f32[4]{0:T(128)S(1)} %get-tuple-element.44, f32[4]{0:T(128)S(1)} %get-tuple-element.45, f32[4,512,128]{2,1,0:T(8,128)S(1)} %fusion.108, f32[4]{0:T(128)S(1)} %get-tuple-element.46, f32[4]{0:T(128)S(1)} %get-tuple-element.47, ...), kind=kOutput, calls=%fused_computation.146 | convolution fusion | flops 1619001344 | bytes 10486368 | tf_op jit(solution)/shard_map/cjk,ckb->cjb/dot_general | solution.py:70
  504.3 3.9 fusion.22
  508.3 3.9 fusion.21
  512.2 4.4 fusion.106
  516.6 4.1 fusion.100
  520.7 4.1 fusion.19
  524.8 4.1 fusion.20
  528.9 4.4 fusion.102
  533.3 4.5 multiply_add_fusion.6
  537.8 3.9 fusion.17
  541.7 4.2 fusion.18
  545.9 4.0 fusion.98
  549.9 4.0 fusion.92
  553.9 4.5 fusion.16
  558.4 4.1 fusion.15
  562.6 4.2 fusion.94
  566.8 4.3 fusion.87
  571.1 4.2 fusion.13
  575.4 4.2 fusion.14
  579.6 8.4 %fusion.114 = f32[4,512,128]{2,1,0:T(8,128)S(1)} fusion(f32[4,512,128]{2,1,0:T(8,128)S(1)} %fusion.94, f32[4,512,128]{2,1,0:T(8,128)S(1)} %fusion.14, bf16[4,512,512]{2,1,0:T(8,128)(2,1)S(1)} %copy-done.3, f32[4,512,128]{2,1,0:T(8,128)S(1)} %get-tuple-element.34, f32[4,512,128]{2,1,0:T(8,128)S(1)} %get-tuple-element.30, f32[4]{0:T(128)S(1)} %get-tuple-element.35, ...), kind=kOutput, calls=%fused_computation.126 | convolution fusion | flops 1621622784 | bytes 11535040 | tf_op jit(solution)/shard_map/cjk,ckb->cjb/dot_general | solution.py:67
  588.0 9.0 %fusion.118 = (f32[4,128]{1,0:T(4,128)S(1)}, f32[4,512,128]{2,1,0:T(8,128)S(1)}) fusion(f32[4,512,128]{2,1,0:T(8,128)S(1)} %fusion.114, f32[512,4,128]{2,0,1:T(8,128)S(1)} %copy-done.5, pred[512]{0:T(512)(128)(4,1)S(1)} %compare_and_fusion, f32[4,512,128]{2,1,0:T(8,128)S(1)} %fusion.87, f32[4]{0:T(128)S(1)} %get-tuple-element.48, ...), kind=kOutput, calls=%fused_computation.133 | convolution fusion | flops 1622670848 | bytes 12585664 | tf_op jit(solution)/shard_map/cjk,ckb->cjb/dot_general | solution.py:70
  597.0 0.2 fusion.127
  597.3 1.1 pad_maximum_fusion.4
  598.3 0.0 all-gather.2.cloned.1.call-update
  598.4 35.3 %all-gather.2.cloned.1.call-done = bf16[4,2,512,512]{3,2,0,1:T(8,128)(2,1)} async-done(((bf16[4,2,512,128]{3,2,0,1:T(8,128)(2,1)}), bf16[4,2,512,512]{3,2,0,1:T(8,128)(2,1)}) %all-gather.2.cloned.1.call-update) | async-done | bytes 4194320 | tf_op jit(solution)/shard_map/all_gather | solution.py:86
  633.7 2.7 slice_bitcast_fusion
  636.3 0.8 copy-done.4
  637.1 0.1 fusion.169
  637.3 2.3 maximum_bitcast_fusion
  639.6 14.0 %fusion.5 = bf16[4,1024,2,512]{3,1,2,0:T(8,128)(2,1)} fusion(bf16[4,512,1024]{2,1,0:T(8,128)(2,1)} %bitcast.119, bf16[4,512,1024]{2,1,0:T(8,128)(2,1)} %bitcast.117, bf16[4,1024,1,512]{3,1,0,2:T(8,128)(2,1)} %get-tuple-element.26, bf16[4,1024,1,512]{3,1,0,2:T(8,128)(2,1)S(1)} %get-tuple-element.25), kind=kOutput, calls=%fused_computation.12 | convolution fusion | flops 8615100416 | bytes 25165824 | tf_op jit(solution)/shard_map/cat,cakb->ctkb/dot_general | solution.py:96
  653.5 16.5 %copy.31 = bf16[4,1024,2,512]{3,2,1,0:T(2,128)(2,1)} copy(bf16[4,1024,2,512]{3,1,2,0:T(8,128)(2,1)} %fusion.5) | data formatting | bytes 16777216 | tf_op jit(solution)/shard_map/convert_element_type | solution.py:97
  (14 shorter events, 0.1 us)
Async XLA Ops:
  6.5 263.1 %copy-start = (f32[4,512,128]{2,1,0:T(8,128)S(1)}, f32[4,512,128]{2,1,0:T(8,128)}, u32[]{:S(2)}) copy-start(f32[4,512,128]{2,1,0:T(8,128)} %param.7) | copy-start | bytes 3145732
  6.5 347.4 %all-reduce.3.cloned.1.call-start = ((), (), s32[]{:S(2)}) async-start(), calls=%async_computation.2 | async-start | bytes 8388608 | tf_op jit(solution)/shard_map/psum | solution.py:45
  268.9 0.7 copy-start.6
  269.0 364.7 %all-gather.2.cloned.1.call-start = ((), (), s32[]{:S(2)}) async-start(), calls=%async_computation.1 | async-start | bytes 5242880 | tf_op jit(solution)/shard_map/all_gather | solution.py:86
  360.2 66.3 %copy-start.2 = (bf16[4,512,512]{2,1,0:T(8,128)(2,1)S(1)}, bf16[4,512,512]{2,1,0:T(8,128)(2,1)}, u32[]{:S(2)}) copy-start(bf16[4,512,512]{2,1,0:T(8,128)(2,1)} %get-tuple-element.5) | copy-start | bytes 6291460
  435.1 9.2 %copy-start.3 = (bf16[4,512,512]{2,1,0:T(8,128)(2,1)S(1)}, bf16[4,512,512]{2,1,0:T(8,128)(2,1)}, u32[]{:S(2)}) copy-start(bf16[4,512,512]{2,1,0:T(8,128)(2,1)} %get-tuple-element.6) | copy-start | bytes 6291460
  435.1 9.2 %copy-start.5 = (f32[512,4,128]{2,0,1:T(8,128)S(1)}, f32[512,4,128]{2,0,1:T(8,128)}, u32[]{:S(2)}) copy-start(f32[512,4,128]{2,0,1:T(8,128)} %gather_fusion) | copy-start | bytes 3145732
  633.7 3.4 copy-start.4
  653.5 16.5 %copy-start.1 = (f32[4,512,128]{2,1,0:T(8,128)S(1)}, f32[4,512,128]{2,1,0:T(8,128)}, u32[]{:S(2)}) copy-start(f32[4,512,128]{2,1,0:T(8,128)} %param.7) | copy-start | bytes 3145732
Sparse Core Ops, SparseCore 0:
  269.1 84.7 all-reduce.2
  598.5 35.1 all-gather.1
where the time goes:
time: 687 us; the launch traced here: 677 us
  matrix products  220 us (32%)
  blocking collectives  192 us (28%)
  local copies, waits for them, and re-layouts  116 us (17%)
  waiting for transfers between devices  116 us (17%)
  other arithmetic  19.3 us (3%)
  between operations  14.1 us (2%)
    all_to_all x1, blocking collectives, local(): lax.all_to_all(spectra, 'chan', split_axis=1, concat_axis=2, tiled=True)  192 us
    psum x1, waiting for transfers between devices, local(): lax.psum(part_imag.astype(jnp.bfloat16), 'tm').astype(jnp.float32)  80.9 us
    div x1, local copies, waits for them, and re-layouts, local(): cov_real = cov_real / spectra_total  60.3 us
    dot_general x7, matrix products, local(): jnp.einsum('cjk,ckb->cjb', cov_real, dir_imag, precision=high)  48.5 us
    dot_general x7, matrix products, local(): jnp.einsum('cjk,ckb->cjb', cov_real, dir_real, precision=high)  47.4 us
    dot_general x7, matrix products, local(): jnp.einsum('cjk,ckb->cjb', cov_imag, dir_imag, precision=high)  37.5 us
    dot_general x7, matrix products, local(): jnp.einsum('cjk,ckb->cjb', cov_imag, dir_real, precision=high)  36.9 us
    all_gather x1, waiting for transfers between devices, local(): block_part = lax.all_gather(weights, 'tm', axis=3, tiled=True)  35.3 us
  transfers between devices with their start and end apart: 2, of which 2 were waited for; matrix products, arithmetic and copies ran while one was open for 1% of the time, Pallas kernels for 0%

commit v1 on v0

v1 whole, which is shorter than its diff:
```python
import math

import jax
import jax.numpy as jnp
from jax import lax
from jax.sharding import PartitionSpec as P

ITERS = 8


def dft_table(count):
    index = jnp.arange(count, dtype=jnp.int32)
    turns = (index[:, None] * index[None, :] % count).astype(jnp.float32)
    angle_grid = 2.0 * math.pi * turns / count
    cosine = jnp.cos(angle_grid)
    sine = jnp.sin(angle_grid)
    upper = jnp.concatenate((cosine, sine), axis=1)
    lower = jnp.concatenate((-sine, cosine), axis=1)
    table = jnp.concatenate((upper, lower), axis=0).astype(jnp.bfloat16)
    return table.reshape(2, count, 2 * count).transpose(1, 0, 2).reshape(2 * count, 2 * count)


def chebyshev(cov_real, cov_imag, steer_real, steer_imag):
    high = lax.Precision.HIGHEST
    stations = cov_real.shape[1]
    loading = jnp.sum(jnp.diagonal(cov_real, axis1=1, axis2=2), axis=1) / stations
    row_mass = jnp.sum(jnp.sqrt(cov_real * cov_real + cov_imag * cov_imag), axis=2)
    bound = loading + jnp.max(row_mass, axis=1)
    center = ((bound + loading) / 2.0)[:, None, None]
    radius = ((bound - loading) / 2.0)[:, None, None]
    eye = jnp.eye(stations, dtype=jnp.float32)
    loaded = cov_real + loading[:, None, None] * eye
    block = jnp.concatenate(
        (
            jnp.concatenate((loaded, -cov_imag), axis=2),
            jnp.concatenate((cov_imag, loaded), axis=2),
        ),
        axis=1,
    )
    steer = jnp.concatenate((steer_real, steer_imag), axis=1)
    res = steer
    dirn = res / center
    sol = jnp.zeros_like(steer)
    rho = radius / center

    def body(_, carry):
        sol, res, dirn, rho = carry
        sol = sol + dirn
        img = jnp.einsum("cjk,ckb->cjb", block, dirn, precision=high)
        res = res - img
        rho_next = 1.0 / (2.0 * center / radius - rho)
        dirn = rho_next * rho * dirn + 2.0 * rho_next / radius * res
        return sol, res, dirn, rho_next

    sol, _, _, _ = lax.fori_loop(0, ITERS, body, (sol, res, dirn, rho))
    response = jnp.sum(steer * sol, axis=1, keepdims=True)
    weights = (sol / response).astype(jnp.bfloat16)
    return weights.reshape(weights.shape[0], 2, stations, weights.shape[2])


def local(samples, station_gain, station_map, steer_phase):
    count = samples.shape[1]
    row_count = samples.shape[2]
    spec_count = samples.shape[3]
    chan_size = lax.axis_size("chan")
    tm_size = lax.axis_size("tm")
    channelized = jnp.dot(
        dft_table(count), samples.reshape(2 * count, -1), preferred_element_type=jnp.float32
    )
    channelized = channelized.reshape(count, 2, row_count, spec_count)
    spectra = (channelized * station_gain[None, None, :, None]).astype(jnp.bfloat16)
    owned = lax.all_to_all(spectra, "chan", split_axis=0, concat_axis=2, tiled=True)
    chans = owned.shape[0]
    stations = owned.shape[2]
    stacked = owned.reshape(chans, 2 * stations, spec_count)
    spectra_total = spec_count * tm_size
    gram_sum = jnp.einsum("cat,cbt->cab", stacked, stacked, preferred_element_type=jnp.float32)
    part_real = gram_sum[:, :stations, :stations] + gram_sum[:, stations:, stations:]
    part_imag = gram_sum[:, stations:, :stations] - gram_sum[:, :stations, stations:]
    part = jnp.stack((part_real, part_imag), axis=1).astype(jnp.bfloat16)
    if chans % tm_size == 0:
        cov = lax.psum_scatter(part, "tm", scatter_dimension=0, tiled=True).astype(jnp.float32)
        phase = lax.all_to_all(steer_phase, "tm", split_axis=0, concat_axis=2, tiled=True)
    else:
        cov = lax.psum(part, "tm").astype(jnp.float32)
        phase = steer_phase
    cov = cov / spectra_total
    phase_rows = jnp.take(phase, station_map, axis=1)
    weights = chebyshev(cov[:, 0], cov[:, 1], jnp.cos(phase_rows), jnp.sin(phase_rows))
    if chans % tm_size == 0:
        weights = lax.all_gather(weights, "tm", axis=0, tiled=True)
    else:
        weights = lax.all_gather(weights, "tm", axis=3, tiled=True)
    weight_real = weights[:, 0]
    weight_imag = weights[:, 1]
    weight_cat = jnp.stack(
        (
            jnp.concatenate((weight_real, weight_imag), axis=1),
            jnp.concatenate((-weight_imag, weight_real), axis=1),
        ),
        axis=2,
    )
    formed = jnp.einsum("cat,cakb->ctkb", stacked, weight_cat, preferred_element_type=jnp.float32)
    return formed.astype(jnp.bfloat16)


def solution(mesh):
    in_specs = (
        P(None, None, ("groups", "chan"), "tm"),
        P(("groups", "chan")),
        P("groups"),
        P("chan", None, ("groups", "tm")),
    )
    out_specs = P("chan", "tm", None, "groups")
    return jax.shard_map(local, mesh=mesh, in_specs=in_specs, out_specs=out_specs, check_vma=False)
```

time: 687 us -> 563 us (0.82); the launches traced: 677 us -> 562 us
  matrix products: 220 us -> 130 us
  local copies, waits for them, and re-layouts: 116 us -> 73.8 us
  other arithmetic: 19.3 us -> 40 us
  waiting for transfers between devices: 116 us -> 107 us
    dot_general x29 -> x9, matrix products: 188 us -> 97.2 us  [the longest x8 80.2 us: body(): img = jnp.einsum('cjk,ckb->cjb', block, dirn, precision=high)]
    psum x1 -> x0, waiting for transfers between devices: 80.9 us -> none  [local(): lax.psum(part_imag.astype(jnp.bfloat16), 'tm').astype(jnp.float32)]
    div x1 -> x0, local copies, waits for them, and re-layouts: 60.3 us -> none  [local(): cov_real = cov_real / spectra_total]
    unnamed x2 -> x3, waiting for transfers between devices: 0.03 us -> 47.4 us
    all_to_all x0 -> x1, waiting for transfers between devices: none -> 24.6 us  [local(): lax.all_to_all(steer_phase, 'tm', split_axis=0, concat_axis=2, tiled=True)]
    while x0 -> x24, local copies, waits for them, and re-layouts: none -> 22.5 us
    concatenate x2 -> x5, other arithmetic: 0.09 us -> 9.56 us  [the longest x2 7.11 us: chebyshev(): steer = jnp.concatenate((steer_real, steer_imag), axis=1)]
    another operation x4, other arithmetic: 1.43 us -> 9.17 us  [the longest x2 9.05 us: local(): part = jnp.stack((part_real, part_imag), axis=1).astype(jnp.bfloat16)]
  transfers between devices with their start and end apart: 2 -> 3, of which waited for: 2 -> 3; matrix products, arithmetic and copies ran while one was open for 1% -> 3% of each run, Pallas kernels for 0% -> 0%
where the time goes in v1:
time: 563 us; the launch traced here: 562 us
  blocking collectives  192 us (34%)
  matrix products  130 us (23%)
  waiting for transfers between devices  107 us (19%)
  local copies, waits for them, and re-layouts  73.8 us (13%)
  other arithmetic  40 us (7%)
  between operations  15.1 us (3%)
    all_to_all x1, blocking collectives, local(): lax.all_to_all(spectra, 'chan', split_axis=0, concat_axis=2, tiled=True)  192 us
    dot_general x8, matrix products, body(): img = jnp.einsum('cjk,ckb->cjb', block, dirn, precision=high)  80.2 us
    unnamed x3, waiting for transfers between devices  47.4 us
    all_gather x1, waiting for transfers between devices, local(): weights = lax.all_gather(weights, 'tm', axis=0, tiled=True)  34.8 us
    all_to_all x1, waiting for transfers between devices, local(): lax.all_to_all(steer_phase, 'tm', split_axis=0, concat_axis=2, tiled=True)  24.6 us
    while x24, local copies, waits for them, and re-layouts  22.5 us
    dot_general x1, matrix products, local(): jnp.dot(dft_table(count), samples.reshape(2 * count, -1), preferred_eleme...  17.5 us
    dot_general x1, matrix products, local(): jnp.einsum('cat,cbt->cab', stacked, stacked, preferred_element_type=jnp.f...  17 us
  transfers between devices with their start and end apart: 3, of which 3 were waited for; matrix products, arithmetic and copies ran while one was open for 3% of the time, Pallas kernels for 0%

profile of v1, /device:TPU:0, one launch (start us, length us, event | category | flops | bytes accessed | tf_op | source)
XLA Modules:
  0.0 562.4 jit_solution(14896484427598856450)
XLA Ops:
  6.5 0.1 negate_convert_fusion
  6.7 0.1 maximum_maximum_fusion.1
  6.7 17.5 %multiply_convert_fusion = bf16[16,2,128,1024]{3,0,2,1:T(8,128)(2,1)} fusion(f32[128]{0:T(128)} %param.7, bf16[16,2,32,1]{2,0,3,1:T(8,128)(2,1)S(1)} %bitcast.141, bf16[4,8,128,1024]{3,2,1,0:T(8,128)(2,1)} %bitcast.142), kind=kOutput, calls=%fused_computation.8 | convolution fusion | flops 276824064 | bytes 16779776 | tf_op jit(solution)/shard_map/dot_general | solution.py:67
  24.3 11.3 %copy.19 = bf16[16,2,128,1024]{3,2,1,0:T(8,128)(2,1)} copy(bf16[16,2,128,1024]{3,0,2,1:T(8,128)(2,1)} %multiply_convert_fusion) | data formatting | bytes 16777216 | tf_op jit(solution)/shard_map/convert_element_type | solution.py:71
  35.6 192.3 %all_to_all.33 = bf16[16,2,128,1024]{3,2,1,0:T(8,128)(2,1)} all-to-all(bf16[16,2,128,1024]{3,2,1,0:T(8,128)(2,1)} %copy.19), channel_id=1, replica_groups=mesh['groups'=2,'chan'=4,'tm'=4] {'chan'}, dimensions={0} | all-to-all | bytes 16777216 | tf_op jit(solution)/shard_map/all_to_all | solution.py:72
  227.9 8.4 %copy.20 = bf16[4,4,2,128,1024]{4,3,0,2,1:T(8,128)(2,1)} copy(bf16[4,4,2,128,1024]{4,3,2,1,0:T(8,128)(2,1)} %bitcast.135) | data formatting | bytes 16777216 | tf_op jit(solution)/shard_map/all_to_all | solution.py:72
  236.3 17.0 %fusion.36 = f32[4,1024,1024]{2,1,0:T(8,128)} fusion(bf16[4,1024,1024]{2,1,0:T(8,128)(2,1)} %bitcast.136), kind=kOutput, calls=%fused_computation.71 | convolution fusion | flops 8589934592 | bytes 25165824 | tf_op jit(solution)/shard_map/cat,cbt->cab/dot_general | solution.py:77
  253.2 6.7 %fusion.18 = (bf16[4,1,512,512]{3,2,0,1:T(8,128)(2,1)S(1)}, bf16[4,1,512,512]{3,2,0,1:T(8,128)(2,1)S(1)}) fusion(f32[4,1024,1024]{2,1,0:T(8,128)} %fusion.36), kind=kLoop, calls=%fused_computation.25 | loop fusion | flops 4194304 | bytes 20971520 | tf_op jit(solution)/shard_map/stack | solution.py:80
  260.0 2.3 pad_maximum_fusion
  262.3 3.5 all-to-all-start.1
  265.9 0.3 all-gather.2.cloned.1.call-start
  266.2 0.6 dynamic-slice
  266.9 24.6 %all-to-all-done.1 = f32[4,512,128]{2,1,0:T(8,128)S(1)} async-done(((f32[4,512,128]{2,1,0:T(8,128)}), f32[4,512,128]{2,1,0:T(8,128)S(1)}, u32[]{:S(2)}, u32[]{:S(2)}) %all-to-all-start.1) | async-done | bytes 1048608 | tf_op jit(solution)/shard_map/all_to_all | solution.py:83
  291.4 0.7 copy.21
  292.1 0.1 copy.45
  292.2 2.3 gather_fusion
  294.5 6.5 %fusion.24 = (f32[1,512,512]{2,1,0:T(8,128)S(1)}, f32[1,512,512]{2,1,0:T(8,128)S(1)}) fusion(f32[512,512]{1,0:T(8,128)} %gather_fusion, pred[512]{0:T(512)(128)(4,1)S(1)} %compare_and_fusion), kind=kLoop, calls=%fused_computation.47 | loop fusion | flops 262144 | bytes 3146240 | tf_op jit(solution)/shard_map/cos | solution.py:89
  301.1 1.0 copy-done.4
  302.1 1.5 pad_maximum_fusion.1
  303.6 5.6 cosine_bitcast_fusion
  309.2 47.3 %all-reduce.3.cloned.1.call-done = bf16[4,2,512,512]{3,2,0,1:T(8,128)(2,1)} async-done(((bf16[4,2,512,512]{3,2,0,1:T(8,128)(2,1)}), bf16[4,2,512,512]{3,2,0,1:T(8,128)(2,1)}) %all-reduce.3.cloned.1.call-update) | async-done | bytes 4194320
  356.5 2.1 convert_multiply_fusion
  358.7 1.3 copy-done.1
  360.0 1.1 slice_bitcast_fusion.2
  361.1 4.5 gather_fusion.1
  365.7 0.7 reduce.5
  366.9 3.3 fusion.34
  370.2 0.6 reduce_max.11
  371.8 2.9 maximum_divide_fusion
  374.6 2.4 maximum_maximum_fusion
  377.0 103.5 %while.19 = (s32[]{:T(128)}, f32[1,1024,512]{2,1,0:T(8,128)S(1)}, f32[1,1024,512]{2,1,0:T(8,128)}, f32[1,1024,512]{2,1,0:T(8,128)}, f32[1,1,1]{2,1,0:T(1,128)}, ...) while((s32[]{:T(128)}, f32[1,1024,512]{2,1,0:T(8,128)S(1)}, ...), condition=%wide.region_5.6_spmd.clone, body=%wide.region_4.5_spmd.clone.sunk | while | flops 6445596672 | bytes 37748964 | solution.py:55
  377.1 1.7 copy.63
  378.9 1.1 copy-done
  379.9 10.0 %multiply_add_fusion.2 = (f32[1,1024,512]{2,1,0:T(8,128)}, f32[1,1024,512]{2,1,0:T(8,128)S(1)}, f32[1,1024,512]{2,1,0:T(8,128)}) fusion(f32[1,1024,512]{2,1,0:T(8,128)S(1)} %copy.63, f32[]{:T(128)} %bitcast.131, f32[]{:T(128)} %bitcast.132, f32[1,1024,512]{2,1,0:T(8,128)S(1)} %get-tuple-element.233, pred[]{:T(512)S(6)} %compare.4, ...), kind=kOutput, calls=%fused_computation.7.clone.1 | convolution fusion | flops 6445596672 | bytes 16777224 | tf_op jit(solution)/shard_map/while/body/eval_jaxpr/cjk,ckb->cjb/dot_general | solution.py:49
  390.0 1.7 copy.63
  391.8 1.1 copy-done
  392.9 10.0 %multiply_add_fusion.2 = (f32[1,1024,512]{2,1,0:T(8,128)}, f32[1,1024,512]{2,1,0:T(8,128)S(1)}, f32[1,1024,512]{2,1,0:T(8,128)}) fusion(f32[1,1024,512]{2,1,0:T(8,128)S(1)} %copy.63, f32[]{:T(128)} %bitcast.131, f32[]{:T(128)} %bitcast.132, f32[1,1024,512]{2,1,0:T(8,128)S(1)} %get-tuple-element.233, pred[]{:T(512)S(6)} %compare.4, ...), kind=kOutput, calls=%fused_computation.7.clone.1 | convolution fusion | flops 6445596672 | bytes 16777224 | tf_op jit(solution)/shard_map/while/body/eval_jaxpr/cjk,ckb->cjb/dot_general | solution.py:49
  403.0 1.7 copy.63
  404.7 1.1 copy-done
  405.8 10.0 %multiply_add_fusion.2 = (f32[1,1024,512]{2,1,0:T(8,128)}, f32[1,1024,512]{2,1,0:T(8,128)S(1)}, f32[1,1024,512]{2,1,0:T(8,128)}) fusion(f32[1,1024,512]{2,1,0:T(8,128)S(1)} %copy.63, f32[]{:T(128)} %bitcast.131, f32[]{:T(128)} %bitcast.132, f32[1,1024,512]{2,1,0:T(8,128)S(1)} %get-tuple-element.233, pred[]{:T(512)S(6)} %compare.4, ...), kind=kOutput, calls=%fused_computation.7.clone.1 | convolution fusion | flops 6445596672 | bytes 16777224 | tf_op jit(solution)/shard_map/while/body/eval_jaxpr/cjk,ckb->cjb/dot_general | solution.py:49
  415.9 1.7 copy.63
  417.7 1.1 copy-done
  418.7 10.0 %multiply_add_fusion.2 = (f32[1,1024,512]{2,1,0:T(8,128)}, f32[1,1024,512]{2,1,0:T(8,128)S(1)}, f32[1,1024,512]{2,1,0:T(8,128)}) fusion(f32[1,1024,512]{2,1,0:T(8,128)S(1)} %copy.63, f32[]{:T(128)} %bitcast.131, f32[]{:T(128)} %bitcast.132, f32[1,1024,512]{2,1,0:T(8,128)S(1)} %get-tuple-element.233, pred[]{:T(512)S(6)} %compare.4, ...), kind=kOutput, calls=%fused_computation.7.clone.1 | convolution fusion | flops 6445596672 | bytes 16777224 | tf_op jit(solution)/shard_map/while/body/eval_jaxpr/cjk,ckb->cjb/dot_general | solution.py:49
  428.9 1.7 copy.63
  430.6 1.1 copy-done
  431.7 10.0 %multiply_add_fusion.2 = (f32[1,1024,512]{2,1,0:T(8,128)}, f32[1,1024,512]{2,1,0:T(8,128)S(1)}, f32[1,1024,512]{2,1,0:T(8,128)}) fusion(f32[1,1024,512]{2,1,0:T(8,128)S(1)} %copy.63, f32[]{:T(128)} %bitcast.131, f32[]{:T(128)} %bitcast.132, f32[1,1024,512]{2,1,0:T(8,128)S(1)} %get-tuple-element.233, pred[]{:T(512)S(6)} %compare.4, ...), kind=kOutput, calls=%fused_computation.7.clone.1 | convolution fusion | flops 6445596672 | bytes 16777224 | tf_op jit(solution)/shard_map/while/body/eval_jaxpr/cjk,ckb->cjb/dot_general | solution.py:49
  441.8 1.7 copy.63
  443.5 1.1 copy-done
  444.6 10.0 %multiply_add_fusion.2 = (f32[1,1024,512]{2,1,0:T(8,128)}, f32[1,1024,512]{2,1,0:T(8,128)S(1)}, f32[1,1024,512]{2,1,0:T(8,128)}) fusion(f32[1,1024,512]{2,1,0:T(8,128)S(1)} %copy.63, f32[]{:T(128)} %bitcast.131, f32[]{:T(128)} %bitcast.132, f32[1,1024,512]{2,1,0:T(8,128)S(1)} %get-tuple-element.233, pred[]{:T(512)S(6)} %compare.4, ...), kind=kOutput, calls=%fused_computation.7.clone.1 | convolution fusion | flops 6445596672 | bytes 16777224 | tf_op jit(solution)/shard_map/while/body/eval_jaxpr/cjk,ckb->cjb/dot_general | solution.py:49
  454.7 1.7 copy.63
  456.5 1.1 copy-done
  457.5 10.0 %multiply_add_fusion.2 = (f32[1,1024,512]{2,1,0:T(8,128)}, f32[1,1024,512]{2,1,0:T(8,128)S(1)}, f32[1,1024,512]{2,1,0:T(8,128)}) fusion(f32[1,1024,512]{2,1,0:T(8,128)S(1)} %copy.63, f32[]{:T(128)} %bitcast.131, f32[]{:T(128)} %bitcast.132, f32[1,1024,512]{2,1,0:T(8,128)S(1)} %get-tuple-element.233, pred[]{:T(512)S(6)} %compare.4, ...), kind=kOutput, calls=%fused_computation.7.clone.1 | convolution fusion | flops 6445596672 | bytes 16777224 | tf_op jit(solution)/shard_map/while/body/eval_jaxpr/cjk,ckb->cjb/dot_general | solution.py:49
  467.7 1.7 copy.63
  469.4 1.1 copy-done
  470.5 10.0 %multiply_add_fusion.2 = (f32[1,1024,512]{2,1,0:T(8,128)}, f32[1,1024,512]{2,1,0:T(8,128)S(1)}, f32[1,1024,512]{2,1,0:T(8,128)}) fusion(f32[1,1024,512]{2,1,0:T(8,128)S(1)} %copy.63, f32[]{:T(128)} %bitcast.131, f32[]{:T(128)} %bitcast.132, f32[1,1024,512]{2,1,0:T(8,128)S(1)} %get-tuple-element.233, pred[]{:T(512)S(6)} %compare.4, ...), kind=kOutput, calls=%fused_computation.7.clone.1 | convolution fusion | flops 6445596672 | bytes 16777224 | tf_op jit(solution)/shard_map/while/body/eval_jaxpr/cjk,ckb->cjb/dot_general | solution.py:49
  480.5 1.5 multiply_reduce_fusion
  482.0 1.3 divide_convert_fusion
  483.3 34.8 %all-gather.2.cloned.1.call-done = bf16[4,2,512,512]{3,2,0,1:T(8,128)(2,1)} async-done(((bf16[1,2,512,512]{3,2,0,1:T(8,128)(2,1)}), bf16[4,2,512,512]{3,2,0,1:T(8,128)(2,1)}) %all-gather.2.cloned.1.call-update) | async-done | bytes 4194320 | tf_op jit(solution)/shard_map/all_gather | solution.py:91
  518.1 2.7 slice_bitcast_fusion
  520.8 0.8 copy-done.3
  521.6 0.1 fusion.35
  521.7 2.3 maximum_bitcast_fusion
  524.0 15.2 %fusion.13 = bf16[4,1024,2,512]{3,1,2,0:T(8,128)(2,1)} fusion(bf16[4,1024,1024,1]{2,1,3,0:T(8,128)(2,1)} %bitcast.137, bf16[4,1024,1,512]{3,1,2,0:T(8,128)(2,1)} %get-tuple-element.153, bf16[4,1024,1,512]{3,1,2,0:T(8,128)(2,1)S(1)} %get-tuple-element.152), kind=kOutput, calls=%fused_computation.16 | convolution fusion | flops 8610906112 | bytes 25165824 | tf_op jit(solution)/shard_map/cat,cakb->ctkb/dot_general | solution.py:103
  539.1 16.4 %copy.25 = bf16[4,1024,2,512]{3,2,1,0:T(2,128)(2,1)} copy(bf16[4,1024,2,512]{3,1,2,0:T(8,128)(2,1)} %fusion.13) | data formatting | bytes 16777216 | tf_op jit(solution)/shard_map/convert_element_type | solution.py:104
  (38 shorter events, 0.2 us)
Async XLA Ops:
  6.5 350.0 %all-reduce.3.cloned.1.call-start = ((), (), s32[]{:S(2)}) async-start(), calls=%async_computation.3 | async-start | bytes 8388608
  262.3 3.9 copy-start.12
  262.3 4.5 copy-start.11
  262.3 29.1 %all-to-all-start.1 = ((f32[4,512,128]{2,1,0:T(8,128)}), f32[4,512,128]{2,1,0:T(8,128)S(1)}, u32[]{:S(2)}, u32[]{:S(2)}) async-start(f32[4,512,128]{2,1,0:T(8,128)} %param.9), calls=%async_computation.1 | async-start | bytes 2097152 | tf_op jit(solution)/shard_map/all_to_all | solution.py:83
  265.9 252.3 %all-gather.2.cloned.1.call-start = ((), (), s32[]{:S(2)}) async-start(), calls=%async_computation.2 | async-start | bytes 5242880 | tf_op jit(solution)/shard_map/all_gather | solution.py:91
  294.5 9.1 %copy-start.2 = (f32[512,512]{1,0:T(8,128)S(1)}, f32[512,512]{1,0:T(8,128)}, u32[]{:S(2)}) copy-start(f32[512,512]{1,0:T(8,128)} %gather_fusion) | copy-start | bytes 3145732
  301.1 1.0 copy-start.4
  301.1 2.5 copy-start.6
  358.7 1.3 copy-start.1
  365.7 6.1 %copy-start.7 = (f32[1,512,512]{2,1,0:T(8,128)S(1)}, f32[1,512,512]{2,1,0:T(8,128)}, u32[]{:S(2)}) copy-start(f32[1,512,512]{2,1,0:T(8,128)} %get-tuple-element.159) | copy-start | bytes 3145732
  370.9 3.8 copy-start.8
  370.9 3.8 copy-start.9
  370.9 3.8 copy-start.10
  374.6 105.9 %copy-start.5 = (f32[1,512,512]{2,1,0:T(8,128)S(1)}, f32[1,512,512]{2,1,0:T(8,128)}, u32[]{:S(2)}) copy-start(f32[1,512,512]{2,1,0:T(8,128)} %copy-done.4) | copy-start | bytes 3145732
  377.1 2.8 copy-start
  390.0 2.8 copy-start
  403.0 2.8 copy-start
  415.9 2.8 copy-start
  428.9 2.8 copy-start
  441.8 2.8 copy-start
  454.7 2.8 copy-start
  467.7 2.8 copy-start
  518.1 3.4 copy-start.3
Sparse Core Ops, SparseCore 0:
  262.4 94.0 all-reduce.2
  483.5 34.6 all-gather.1

commit v2 on v1

--- a/solution.py
+++ b/solution.py
@@ -21,7 +21,7 @@
 
 
 def chebyshev(cov_real, cov_imag, steer_real, steer_imag):
-    high = lax.Precision.HIGHEST
+    high = lax.Precision.HIGH
     stations = cov_real.shape[1]
     loading = jnp.sum(jnp.diagonal(cov_real, axis1=1, axis2=2), axis=1) / stations
     row_mass = jnp.sum(jnp.sqrt(cov_real * cov_real + cov_imag * cov_imag), axis=2)
@@ -58,6 +58,22 @@
     return weights.reshape(weights.shape[0], 2, stations, weights.shape[2])
 
 
+def exchange_phase(steer_phase, tm_size):
+    own = lax.axis_index("tm")
+    block = steer_phase.shape[0] // tm_size
+    pieces = steer_phase.reshape(tm_size, block, *steer_phase.shape[1:])
+    received = [lax.dynamic_index_in_dim(pieces, own, 0, keepdims=False)]
+    for shift in range(1, tm_size):
+        target = (own + shift) % tm_size
+        outgoing = lax.dynamic_index_in_dim(pieces, target, 0, keepdims=False)
+        perm = [(j, (j + shift) % tm_size) for j in range(tm_size)]
+        received.append(lax.ppermute(outgoing, "tm", perm))
+    stacked = jnp.stack(received, axis=0)
+    order = (own - jnp.arange(tm_size)) % tm_size
+    ordered = jnp.take(stacked, order, axis=0)
+    return jnp.moveaxis(ordered, 0, 2).reshape(block, steer_phase.shape[1], -1)
+
+
 def local(samples, station_gain, station_map, steer_phase):
     count = samples.shape[1]
     row_count = samples.shape[2]
@@ -69,6 +85,12 @@
     )
     channelized = channelized.reshape(count, 2, row_count, spec_count)
     spectra = (channelized * station_gain[None, None, :, None]).astype(jnp.bfloat16)
+    split_channels = (count // chan_size) % tm_size == 0
+    if split_channels:
+        phase = exchange_phase(steer_phase, tm_size)
+        spectra, phase = lax.optimization_barrier((spectra, phase))
+    else:
+        phase = steer_phase
     owned = lax.all_to_all(spectra, "chan", split_axis=0, concat_axis=2, tiled=True)
     chans = owned.shape[0]
     stations = owned.shape[2]
@@ -77,17 +99,17 @@
     gram_sum = jnp.einsum("cat,cbt->cab", stacked, stacked, preferred_element_type=jnp.float32)
     part_real = gram_sum[:, :stations, :stations] + gram_sum[:, stations:, stations:]
     part_imag = gram_sum[:, stations:, :stations] - gram_sum[:, :stations, stations:]
-    part = jnp.stack((part_real, part_imag), axis=1).astype(jnp.bfloat16)
-    if chans % tm_size == 0:
+    part = jnp.concatenate((part_real, part_imag), axis=1).astype(jnp.bfloat16)
+    if split_channels:
         cov = lax.psum_scatter(part, "tm", scatter_dimension=0, tiled=True).astype(jnp.float32)
-        phase = lax.all_to_all(steer_phase, "tm", split_axis=0, concat_axis=2, tiled=True)
     else:
         cov = lax.psum(part, "tm").astype(jnp.float32)
-        phase = steer_phase
     cov = cov / spectra_total
     phase_rows = jnp.take(phase, station_map, axis=1)
-    weights = chebyshev(cov[:, 0], cov[:, 1], jnp.cos(phase_rows), jnp.sin(phase_rows))
-    if chans % tm_size == 0:
+    weights = chebyshev(
+        cov[:, :stations], cov[:, stations:], jnp.cos(phase_rows), jnp.sin(phase_rows)
+    )
+    if split_channels:
         weights = lax.all_gather(weights, "tm", axis=0, tiled=True)
     else:
         weights = lax.all_gather(weights, "tm", axis=3, tiled=True)

time: 563 us -> 491 us (0.87)
  waiting for transfers between devices: 107 us -> 60.4 us
  matrix products: 130 us -> 105 us
    unnamed x3 -> x2, waiting for transfers between devices: 47.4 us -> 0.03 us
    reduce_scatter x0 -> x1, waiting for transfers between devices: none -> 25.7 us  [local(): lax.psum_scatter(part, 'tm', scatter_dimension=0, tiled=True)]
    dot_general x8, matrix products: 80.2 us -> 55.4 us  [body(): img = jnp.einsum('cjk,ckb->cjb', block, dirn, precision=high)]
    all_to_all x1 -> x0, waiting for transfers between devices: 24.6 us -> none  [local(): lax.all_to_all(steer_phase, 'tm', split_axis=0, concat_axis=2, tiled=True)]
    convert_element_type x1 -> x0, local copies, waits for them, and re-layouts: 11.3 us -> none  [local(): (channelized * station_gain[None, None, :, None]).astype(jnp.bfloat16)]
    optimization_barrier x0 -> x1, local copies, waits for them, and re-layouts: none -> 11.3 us  [local(): spectra, phase = lax.optimization_barrier((spectra, phase))]
  transfers between devices with their start and end apart: 3 -> 5, of which waited for: 3 -> 2; matrix products, arithmetic and copies ran while one was open for 3% -> 7% of each run, Pallas kernels for 0% -> 0%
where the time goes in v2:
time: 491 us; the launch traced here: 490 us
  blocking collectives  190 us (39%)
  matrix products  105 us (21%)
  local copies, waits for them, and re-layouts  73.7 us (15%)
  waiting for transfers between devices  60.4 us (12%)
  other arithmetic  40.3 us (8%)
  between operations  15.1 us (3%)
    all_to_all x1, blocking collectives, local(): lax.all_to_all(spectra, 'chan', split_axis=0, concat_axis=2, tiled=True)  190 us
    dot_general x8, matrix products, body(): img = jnp.einsum('cjk,ckb->cjb', block, dirn, precision=high)  55.4 us
    all_gather x1, waiting for transfers between devices, local(): weights = lax.all_gather(weights, 'tm', axis=0, tiled=True)  34.6 us
    reduce_scatter x1, waiting for transfers between devices, local(): lax.psum_scatter(part, 'tm', scatter_dimension=0, tiled=True)  25.7 us
    while x24, local copies, waits for them, and re-layouts  22.5 us
    dot_general x1, matrix products, local(): jnp.dot(dft_table(count), samples.reshape(2 * count, -1), preferred_eleme...  17.5 us
    dot_general x1, matrix products, local(): jnp.einsum('cat,cbt->cab', stacked, stacked, preferred_element_type=jnp.f...  16.9 us
    convert_element_type x1, local copies, waits for them, and re-layouts, local(): return formed.astype(jnp.bfloat16)  16.4 us
  transfers between devices with their start and end apart: 5, of which 2 were waited for; matrix products, arithmetic and copies ran while one was open for 7% of the time, Pallas kernels for 0%

profile of v2, /device:TPU:0, one launch (start us, length us, event | category | flops | bytes accessed | tf_op | source)
XLA Modules:
  0.0 490.1 jit_solution(7449920032821178134)
XLA Ops:
  6.5 1.3 dynamic-slice_bitcast_fusion
  7.8 0.5 collective-permute-start
  8.3 2.6 collective-permute-start.1
  10.9 1.4 collective-permute-start.2
  12.4 0.1 maximum_maximum_fusion.1
  12.5 17.5 %multiply_convert_fusion = bf16[16,2,128,1024]{3,0,2,1:T(8,128)(2,1)} fusion(f32[128]{0:T(128)} %param.7, bf16[16,2,32,1]{2,0,3,1:T(8,128)(2,1)S(1)} %bitcast.125, bf16[4,8,128,1024]{3,2,1,0:T(8,128)(2,1)} %bitcast.126), kind=kOutput, calls=%fused_computation.9 | convolution fusion | flops 276824064 | bytes 16779776 | tf_op jit(solution)/shard_map/dot_general | solution.py:83
  30.1 0.1 maximum_bitcast_fusion.2
  30.1 0.6 gather_fusion
  30.8 0.2 copy_bitcast_fusion
  31.0 11.3 %copy.18 = bf16[16,2,128,1024]{3,2,1,0:T(8,128)(2,1)} copy(bf16[16,2,128,1024]{3,0,2,1:T(8,128)(2,1)} %multiply_convert_fusion) | data formatting | bytes 16777216 | tf_op jit(solution)/shard_map/optimization_barrier | solution.py:91
  42.3 190.2 %all_to_all.15 = bf16[16,2,128,1024]{3,2,1,0:T(8,128)(2,1)} all-to-all(bf16[16,2,128,1024]{3,2,1,0:T(8,128)(2,1)} %copy.18), channel_id=1, replica_groups=mesh['groups'=2,'chan'=4,'tm'=4] {'chan'}, dimensions={0} | all-to-all | bytes 16777216 | tf_op jit(solution)/shard_map/all_to_all | solution.py:94
  232.5 8.4 %copy.19 = bf16[4,4,2,128,1024]{4,3,0,2,1:T(8,128)(2,1)} copy(bf16[4,4,2,128,1024]{4,3,2,1,0:T(8,128)(2,1)} %bitcast.118) | data formatting | bytes 16777216 | tf_op jit(solution)/shard_map/all_to_all | solution.py:94
  240.9 16.9 %fusion.34 = f32[4,1024,1024]{2,1,0:T(8,128)} fusion(bf16[4,1024,1024]{2,1,0:T(8,128)(2,1)} %bitcast.119), kind=kOutput, calls=%fused_computation.85 | convolution fusion | flops 8589934592 | bytes 25165824 | tf_op jit(solution)/shard_map/cat,cbt->cab/dot_general | solution.py:99
  257.8 6.7 %fusion.17 = (bf16[4,512,512]{2,1,0:T(8,128)(2,1)S(1)}, bf16[4,512,512]{2,1,0:T(8,128)(2,1)S(1)}) fusion(f32[4,1024,1024]{2,1,0:T(8,128)} %fusion.34), kind=kLoop, calls=%fused_computation.21 | loop fusion | flops 4194304 | bytes 20971520 | tf_op jit(solution)/shard_map/convert
  264.5 2.2 pad_maximum_fusion
  266.9 0.6 copy-done.9
  267.5 2.3 gather_fusion.1
  269.8 6.6 %fusion.20 = (f32[1,512,512]{2,1,0:T(8,128)S(1)}, f32[1,512,512]{2,1,0:T(8,128)S(1)}) fusion(f32[512,512]{1,0:T(8,128)} %gather_fusion.1, pred[512]{0:T(512)(128)(4,1)S(1)} %compare_and_fusion), kind=kLoop, calls=%fused_computation.44 | loop fusion | flops 262144 | bytes 3146240 | tf_op jit(solution)/shard_map/cos | solution.py:110
  276.4 0.9 copy-done.4
  277.4 1.5 pad_maximum_fusion.1
  278.9 5.6 %cosine_bitcast_fusion = (f32[1,512,512]{2,1,0:T(8,128)}, f32[1,512,512]{2,1,0:T(8,128)}) fusion(f32[512,512]{1,0:T(8,128)S(1)} %copy-done.2, pred[512]{0:T(512)(128)(4,1)S(1)} %compare_and_fusion), kind=kLoop, calls=%fused_computation.42 | loop fusion | flops 262144 | bytes 3146240 | tf_op jit(solution)/shard_map/concatenate | solution.py:40
  284.5 25.7 %reduce-scatter.2.cloned.1.call-done = bf16[1,1024,512]{2,1,0:T(8,128)(2,1)} async-done(((bf16[4,1024,512]{2,1,0:T(8,128)(2,1)}), bf16[1,1024,512]{2,1,0:T(8,128)(2,1)}) %reduce-scatter.2.cloned.1.call-update) | async-done | bytes 1048592 | tf_op jit(solution)/shard_map/reduce_scatter | solution.py:104
  310.2 1.5 convert_multiply_fusion
  311.7 1.3 copy-done.1
  313.1 4.5 gather_fusion.2
  317.6 0.6 reduce.5
  318.9 3.3 slice_negate_fusion
  322.2 0.7 reduce_max.11
  323.8 4.3 maximum_maximum_fusion
  328.1 1.6 maximum_divide_fusion
  329.7 78.7 %while.19 = (s32[]{:T(128)}, f32[1,1024,512]{2,1,0:T(8,128)S(1)}, f32[1,1024,512]{2,1,0:T(8,128)}, f32[1,1024,512]{2,1,0:T(8,128)}, f32[1,1,1]{2,1,0:T(1,128)}, ...) while((s32[]{:T(128)}, f32[1,1024,512]{2,1,0:T(8,128)S(1)}, ...), condition=%wide.region_5.6_spmd.clone, body=%wide.region_4.5_spmd.clone.sunk | while | flops 3224371200 | bytes 37748964 | solution.py:55
  329.8 1.7 copy.56
  331.5 1.1 copy-done
  332.6 6.9 %multiply_add_fusion.2 = (f32[1,1024,512]{2,1,0:T(8,128)}, f32[1,1024,512]{2,1,0:T(8,128)S(1)}, f32[1,1024,512]{2,1,0:T(8,128)}) fusion(f32[1,1024,512]{2,1,0:T(8,128)S(1)} %copy.56, f32[]{:T(128)} %bitcast.114, f32[]{:T(128)} %bitcast.115, f32[1,1024,512]{2,1,0:T(8,128)S(1)} %get-tuple-element.240, pred[]{:T(512)S(6)} %compare.15, ...), kind=kOutput, calls=%fused_computation.8.clone.1 | convolution fusion | flops 3224371200 | bytes 16777224 | tf_op jit(solution)/shard_map/while/body/eval_jaxpr/cjk,ckb->cjb/dot_general | solution.py:49
  339.6 1.7 copy.56
  341.4 1.1 copy-done
  342.4 6.9 %multiply_add_fusion.2 = (f32[1,1024,512]{2,1,0:T(8,128)}, f32[1,1024,512]{2,1,0:T(8,128)S(1)}, f32[1,1024,512]{2,1,0:T(8,128)}) fusion(f32[1,1024,512]{2,1,0:T(8,128)S(1)} %copy.56, f32[]{:T(128)} %bitcast.114, f32[]{:T(128)} %bitcast.115, f32[1,1024,512]{2,1,0:T(8,128)S(1)} %get-tuple-element.240, pred[]{:T(512)S(6)} %compare.15, ...), kind=kOutput, calls=%fused_computation.8.clone.1 | convolution fusion | flops 3224371200 | bytes 16777224 | tf_op jit(solution)/shard_map/while/body/eval_jaxpr/cjk,ckb->cjb/dot_general | solution.py:49
  349.5 1.7 copy.56
  351.2 1.1 copy-done
  352.3 6.9 %multiply_add_fusion.2 = (f32[1,1024,512]{2,1,0:T(8,128)}, f32[1,1024,512]{2,1,0:T(8,128)S(1)}, f32[1,1024,512]{2,1,0:T(8,128)}) fusion(f32[1,1024,512]{2,1,0:T(8,128)S(1)} %copy.56, f32[]{:T(128)} %bitcast.114, f32[]{:T(128)} %bitcast.115, f32[1,1024,512]{2,1,0:T(8,128)S(1)} %get-tuple-element.240, pred[]{:T(512)S(6)} %compare.15, ...), kind=kOutput, calls=%fused_computation.8.clone.1 | convolution fusion | flops 3224371200 | bytes 16777224 | tf_op jit(solution)/shard_map/while/body/eval_jaxpr/cjk,ckb->cjb/dot_general | solution.py:49
  359.3 1.7 copy.56
  361.0 1.1 copy-done
  362.1 6.9 %multiply_add_fusion.2 = (f32[1,1024,512]{2,1,0:T(8,128)}, f32[1,1024,512]{2,1,0:T(8,128)S(1)}, f32[1,1024,512]{2,1,0:T(8,128)}) fusion(f32[1,1024,512]{2,1,0:T(8,128)S(1)} %copy.56, f32[]{:T(128)} %bitcast.114, f32[]{:T(128)} %bitcast.115, f32[1,1024,512]{2,1,0:T(8,128)S(1)} %get-tuple-element.240, pred[]{:T(512)S(6)} %compare.15, ...), kind=kOutput, calls=%fused_computation.8.clone.1 | convolution fusion | flops 3224371200 | bytes 16777224 | tf_op jit(solution)/shard_map/while/body/eval_jaxpr/cjk,ckb->cjb/dot_general | solution.py:49
  369.1 1.7 copy.56
  370.9 1.1 copy-done
  371.9 6.9 %multiply_add_fusion.2 = (f32[1,1024,512]{2,1,0:T(8,128)}, f32[1,1024,512]{2,1,0:T(8,128)S(1)}, f32[1,1024,512]{2,1,0:T(8,128)}) fusion(f32[1,1024,512]{2,1,0:T(8,128)S(1)} %copy.56, f32[]{:T(128)} %bitcast.114, f32[]{:T(128)} %bitcast.115, f32[1,1024,512]{2,1,0:T(8,128)S(1)} %get-tuple-element.240, pred[]{:T(512)S(6)} %compare.15, ...), kind=kOutput, calls=%fused_computation.8.clone.1 | convolution fusion | flops 3224371200 | bytes 16777224 | tf_op jit(solution)/shard_map/while/body/eval_jaxpr/cjk,ckb->cjb/dot_general | solution.py:49
  379.0 1.7 copy.56
  380.7 1.1 copy-done
  381.8 6.9 %multiply_add_fusion.2 = (f32[1,1024,512]{2,1,0:T(8,128)}, f32[1,1024,512]{2,1,0:T(8,128)S(1)}, f32[1,1024,512]{2,1,0:T(8,128)}) fusion(f32[1,1024,512]{2,1,0:T(8,128)S(1)} %copy.56, f32[]{:T(128)} %bitcast.114, f32[]{:T(128)} %bitcast.115, f32[1,1024,512]{2,1,0:T(8,128)S(1)} %get-tuple-element.240, pred[]{:T(512)S(6)} %compare.15, ...), kind=kOutput, calls=%fused_computation.8.clone.1 | convolution fusion | flops 3224371200 | bytes 16777224 | tf_op jit(solution)/shard_map/while/body/eval_jaxpr/cjk,ckb->cjb/dot_general | solution.py:49
  388.8 1.7 copy.56
  390.6 1.1 copy-done
  391.6 6.9 %multiply_add_fusion.2 = (f32[1,1024,512]{2,1,0:T(8,128)}, f32[1,1024,512]{2,1,0:T(8,128)S(1)}, f32[1,1024,512]{2,1,0:T(8,128)}) fusion(f32[1,1024,512]{2,1,0:T(8,128)S(1)} %copy.56, f32[]{:T(128)} %bitcast.114, f32[]{:T(128)} %bitcast.115, f32[1,1024,512]{2,1,0:T(8,128)S(1)} %get-tuple-element.240, pred[]{:T(512)S(6)} %compare.15, ...), kind=kOutput, calls=%fused_computation.8.clone.1 | convolution fusion | flops 3224371200 | bytes 16777224 | tf_op jit(solution)/shard_map/while/body/eval_jaxpr/cjk,ckb->cjb/dot_general | solution.py:49
  398.7 1.7 copy.56
  400.4 1.1 copy-done
  401.5 6.9 %multiply_add_fusion.2 = (f32[1,1024,512]{2,1,0:T(8,128)}, f32[1,1024,512]{2,1,0:T(8,128)S(1)}, f32[1,1024,512]{2,1,0:T(8,128)}) fusion(f32[1,1024,512]{2,1,0:T(8,128)S(1)} %copy.56, f32[]{:T(128)} %bitcast.114, f32[]{:T(128)} %bitcast.115, f32[1,1024,512]{2,1,0:T(8,128)S(1)} %get-tuple-element.240, pred[]{:T(512)S(6)} %compare.15, ...), kind=kOutput, calls=%fused_computation.8.clone.1 | convolution fusion | flops 3224371200 | bytes 16777224 | tf_op jit(solution)/shard_map/while/body/eval_jaxpr/cjk,ckb->cjb/dot_general | solution.py:49
  408.4 1.5 multiply_reduce_fusion
  409.9 1.3 divide_convert_fusion
  411.2 34.6 %all-gather.2.cloned.1.call-done = bf16[4,2,512,512]{3,2,0,1:T(8,128)(2,1)} async-done(((bf16[1,2,512,512]{3,2,0,1:T(8,128)(2,1)}), bf16[4,2,512,512]{3,2,0,1:T(8,128)(2,1)}) %all-gather.2.cloned.1.call-update) | async-done | bytes 4194320 | tf_op jit(solution)/shard_map/all_gather | solution.py:113
  445.9 2.7 slice_bitcast_fusion
  448.5 0.8 copy-done.3
  449.3 0.1 fusion.33
  449.4 2.3 maximum_bitcast_fusion
  451.7 15.1 %fusion.13 = bf16[4,1024,2,512]{3,1,2,0:T(8,128)(2,1)} fusion(bf16[4,1024,1024,1]{2,1,3,0:T(8,128)(2,1)} %bitcast.120, bf16[4,1024,1,512]{3,1,2,0:T(8,128)(2,1)} %get-tuple-element.157, bf16[4,1024,1,512]{3,1,2,0:T(8,128)(2,1)S(1)} %get-tuple-element.156), kind=kOutput, calls=%fused_computation.17 | convolution fusion | flops 8610906112 | bytes 25165824 | tf_op jit(solution)/shard_map/cat,cakb->ctkb/dot_general | solution.py:125
  466.8 16.4 %copy.22 = bf16[4,1024,2,512]{3,2,1,0:T(2,128)(2,1)} copy(bf16[4,1024,2,512]{3,1,2,0:T(8,128)(2,1)} %fusion.13) | data formatting | bytes 16777216 | tf_op jit(solution)/shard_map/convert_element_type | solution.py:126
  (40 shorter events, 0.4 us)
Async XLA Ops:
  6.5 303.6 %reduce-scatter.2.cloned.1.call-start = ((), (), s32[]{:S(2)}) async-start(), calls=%async_computation.2 | async-start | bytes 5242880 | tf_op jit(solution)/shard_map/reduce_scatter | solution.py:104
  7.8 22.2 %collective-permute-start = (f32[1,512,128]{2,1,0:T(8,128)S(1)}, f32[1,512,128]{2,1,0:T(8,128)S(1)}, u32[]{:S(2)}, u32[]{:S(2)}) collective-permute-start(f32[1,512,128]{2,1,0:T(8,128)S(1)} %get-tuple-element.167), channel_id=1, source_target_pairs={{0,1},{1,2},{2,3},{3,0},{4,5},{5,6},{6,7},{7,4},{8,9},{9,10},{10,1... | collective-permute-start | bytes 786440 | tf_op jit(solution)/shard_map/ppermute | solution.py:70
  8.3 21.7 %collective-permute-start.1 = (f32[1,512,128]{2,1,0:T(8,128)S(1)}, f32[1,512,128]{2,1,0:T(8,128)S(1)}, u32[]{:S(2)}, u32[]{:S(2)}) collective-permute-start(f32[1,512,128]{2,1,0:T(8,128)S(1)} %get-tuple-element.169), channel_id=1, source_target_pairs={{0,2},{1,3},{2,0},{3,1},{4,6},{5,7},{6,4},{7,5},{8,10},{9,11},{10,... | collective-permute-start | bytes 786440 | tf_op jit(solution)/shard_map/ppermute | solution.py:70
  10.9 19.2 %collective-permute-start.2 = (f32[1,512,128]{2,1,0:T(8,128)S(1)}, f32[1,512,128]{2,1,0:T(8,128)S(1)}, u32[]{:S(2)}, u32[]{:S(2)}) collective-permute-start(f32[1,512,128]{2,1,0:T(8,128)S(1)} %get-tuple-element.168), channel_id=1, source_target_pairs={{0,3},{1,0},{2,1},{3,2},{4,7},{5,4},{6,5},{7,6},{8,11},{9,8},{10,9... | collective-permute-start | bytes 786440 | tf_op jit(solution)/shard_map/ppermute | solution.py:70
  266.8 0.7 copy-start.9
  266.8 179.1 %all-gather.2.cloned.1.call-start = ((), (), s32[]{:S(2)}) async-start(), calls=%async_computation.3 | async-start | bytes 5242880 | tf_op jit(solution)/shard_map/all_gather | solution.py:113
  269.8 9.1 %copy-start.2 = (f32[512,512]{1,0:T(8,128)S(1)}, f32[512,512]{1,0:T(8,128)}, u32[]{:S(2)}) copy-start(f32[512,512]{1,0:T(8,128)} %gather_fusion.1) | copy-start | bytes 3145732
  276.4 1.0 copy-start.4
  276.4 2.5 copy-start.6
  311.7 1.3 copy-start.1
  322.8 5.2 %copy-start.7 = (f32[1,512,512]{2,1,0:T(8,128)S(1)}, f32[1,512,512]{2,1,0:T(8,128)}, u32[]{:S(2)}) copy-start(f32[1,512,512]{2,1,0:T(8,128)} %get-tuple-element.162) | copy-start | bytes 3145732
  322.8 5.2 %copy-start.8 = (f32[1,512,512]{2,1,0:T(8,128)S(1)}, f32[1,512,512]{2,1,0:T(8,128)}, u32[]{:S(2)}) copy-start(f32[1,512,512]{2,1,0:T(8,128)} %get-tuple-element.163) | copy-start | bytes 3145732
  328.1 80.3 %copy-start.5 = (f32[1,512,512]{2,1,0:T(8,128)S(1)}, f32[1,512,512]{2,1,0:T(8,128)}, u32[]{:S(2)}) copy-start(f32[1,512,512]{2,1,0:T(8,128)} %copy-done.4) | copy-start | bytes 3145732
  329.8 2.8 copy-start
  339.6 2.8 copy-start
  349.4 2.8 copy-start
  359.3 2.8 copy-start
  369.1 2.8 copy-start
  379.0 2.8 copy-start
  388.8 2.8 copy-start
  398.6 2.8 copy-start
  445.8 3.4 copy-start.3
Sparse Core Ops, SparseCore 0:
  266.9 43.2 reduce-scatter.1
  411.3 34.4 all-gather.1

commit v3 on v1

v3 whole, which is shorter than its diff:
```python
import math

import jax
import jax.numpy as jnp
from jax import lax
from jax.sharding import PartitionSpec as P

ITERS = 8


def full_dft_table(count):
    index = jnp.arange(count, dtype=jnp.int32)
    turns = (index[:, None] * index[None, :] % count).astype(jnp.float32)
    angle_grid = 2.0 * math.pi * turns / count
    cosine = jnp.cos(angle_grid)
    sine = jnp.sin(angle_grid)
    upper = jnp.concatenate((cosine, sine), axis=1)
    lower = jnp.concatenate((-sine, cosine), axis=1)
    return jnp.concatenate((upper, lower), axis=0).astype(jnp.bfloat16)


def chebyshev(cov_real, cov_imag, steer_real, steer_imag):
    high = lax.Precision.HIGH
    stations = cov_real.shape[1]
    loading = jnp.sum(jnp.diagonal(cov_real, axis1=1, axis2=2), axis=1) / stations
    row_mass = jnp.sum(jnp.sqrt(cov_real * cov_real + cov_imag * cov_imag), axis=2)
    bound = loading + jnp.max(row_mass, axis=1)
    center = ((bound + loading) / 2.0)[:, None, None]
    radius = ((bound - loading) / 2.0)[:, None, None]
    eye = jnp.eye(stations, dtype=jnp.float32)
    loaded = cov_real + loading[:, None, None] * eye
    block = jnp.concatenate(
        (
            jnp.concatenate((loaded, -cov_imag), axis=2),
            jnp.concatenate((cov_imag, loaded), axis=2),
        ),
        axis=1,
    )
    steer = jnp.concatenate((steer_real, steer_imag), axis=1)
    res = steer
    dirn = res / center
    sol = jnp.zeros_like(steer)
    rho = radius / center

    def body(_, carry):
        sol, res, dirn, rho = carry
        sol = sol + dirn
        img = jnp.einsum("cjk,ckb->cjb", block, dirn, precision=high)
        res = res - img
        rho_next = 1.0 / (2.0 * center / radius - rho)
        dirn = rho_next * rho * dirn + 2.0 * rho_next / radius * res
        return sol, res, dirn, rho_next

    sol, _, _, _ = lax.fori_loop(0, ITERS, body, (sol, res, dirn, rho))
    response = jnp.sum(steer * sol, axis=1, keepdims=True)
    weights = (sol / response).astype(jnp.bfloat16)
    return weights.reshape(weights.shape[0], 2, stations, weights.shape[2])


def local(samples, station_gain, station_map, steer_phase):
    count = samples.shape[1]
    row_count = samples.shape[2]
    spec_count = samples.shape[3]
    chan_size = lax.axis_size("chan")
    tm_size = lax.axis_size("tm")
    slots = count // chan_size
    here = lax.axis_index("chan")
    stations = chan_size * row_count
    spectra_total = spec_count * tm_size
    table = full_dft_table(count)
    flat = samples.reshape(2 * count, -1)
    gain = station_gain[None, None, :, None]
    source = (here - jnp.arange(chan_size)) % chan_size
    arrival = (source[:, None] * row_count + jnp.arange(row_count)[None, :]).reshape(-1)
    phase_rows = jnp.take(steer_phase, jnp.take(station_map, arrival), axis=1)
    steer_real = jnp.cos(phase_rows)
    steer_imag = jnp.sin(phase_rows)
    previous = None
    beams = []
    for slot in range(slots):
        rows = [part * count + dest * slots + slot for dest in range(chan_size) for part in range(2)]
        channelized = jnp.dot(table[jnp.array(rows)], flat, preferred_element_type=jnp.float32)
        channelized = channelized.reshape(chan_size, 2, row_count, spec_count)
        spectra = (channelized * gain).astype(jnp.bfloat16)
        if previous is not None:
            spectra, _ = lax.optimization_barrier((spectra, previous))
        received = [lax.dynamic_index_in_dim(spectra, here, 0, keepdims=False)]
        for shift in range(1, chan_size):
            outgoing = lax.dynamic_index_in_dim(spectra, (here + shift) % chan_size, 0, keepdims=False)
            perm = [(j, (j + shift) % chan_size) for j in range(chan_size)]
            received.append(lax.ppermute(outgoing, "chan", perm))
        previous = tuple(received)
        stacked = jnp.stack(received, axis=1).reshape(2 * stations, spec_count)
        gram_sum = jnp.dot(stacked, stacked.T, preferred_element_type=jnp.float32)
        part_real = gram_sum[:stations, :stations] + gram_sum[stations:, stations:]
        part_imag = gram_sum[stations:, :stations] - gram_sum[:stations, stations:]
        part = jnp.concatenate((part_real, part_imag), axis=0).astype(jnp.bfloat16)
        if slot > 0:
            part, _ = lax.optimization_barrier((part, reduced))
        reduced = lax.psum(part, "tm")
        cov = reduced.astype(jnp.float32) / spectra_total
        weights = chebyshev(
            cov[None, :stations],
            cov[None, stations:],
            steer_real[slot : slot + 1],
            steer_imag[slot : slot + 1],
        )
        weights = lax.all_gather(weights[0], "tm", axis=2, tiled=True)
        weight_real = weights[0]
        weight_imag = weights[1]
        weight_cat = jnp.stack(
            (
                jnp.concatenate((weight_real, weight_imag), axis=0),
                jnp.concatenate((-weight_imag, weight_real), axis=0),
            ),
            axis=1,
        )
        formed = jnp.einsum("at,akb->tkb", stacked, weight_cat, preferred_element_type=jnp.float32)
        beams.append(formed.astype(jnp.bfloat16))
    return jnp.stack(beams, axis=0)


def solution(mesh):
    in_specs = (
        P(None, None, ("groups", "chan"), "tm"),
        P(("groups", "chan")),
        P("groups"),
        P("chan", None, ("groups", "tm")),
    )
    out_specs = P("chan", "tm", None, "groups")
    return jax.shard_map(local, mesh=mesh, in_specs=in_specs, out_specs=out_specs, check_vma=False)
```

time: 563 us -> 635 us (1.13)
  the two profiles are of different devices: /device:TPU:0 before, /device:TPU:11 now
where the time goes in v3:
time: 635 us; the launch traced here: 624 us
  matrix products  228 us (36%)
  local copies, waits for them, and re-layouts  184 us (29%)
  waiting for transfers between devices  98.4 us (15%)
  other arithmetic  76.8 us (12%)
  between operations  20.1 us (3%)
  starting transfers between devices  13.9 us (2%)
    dot_general x32, matrix products, body(): img = jnp.einsum('cjk,ckb->cjb', block, dirn, precision=high)  144 us
    ppermute x12, waiting for transfers between devices, local(): received.append(lax.ppermute(outgoing, 'chan', perm))  85.1 us
    dot_general x4, matrix products, local(): jnp.dot(table[jnp.array(rows)], flat, preferred_element_type=jnp.float32)  55.5 us
    another operation x1, local copies, waits for them, and re-layouts, local(): return jnp.stack(beams, axis=0)  37.9 us
    reshape x8, local copies, waits for them, and re-layouts, local(): stacked = jnp.stack(received, axis=1).reshape(2 * stations, spec_count)  36 us
    unnamed x88, local copies, waits for them, and re-layouts  28.5 us
    dynamic_slice x4, local copies, waits for them, and re-layouts, local(): received = [lax.dynamic_index_in_dim(spectra, here, 0, keepdims=False)]  27.1 us
    gather x4, local copies, waits for them, and re-layouts, chebyshev(): jnp.diagonal(cov_real, axis1=1, axis2=2)  18.5 us
  transfers between devices with their start and end apart: 20, of which 7 were waited for; matrix products, arithmetic and copies ran while one was open for 60% of the time, Pallas kernels for 0%

profile of v3, /device:TPU:11, one launch (start us, length us, event | category | flops | bytes accessed | tf_op | source)
XLA Modules:
  0.0 624.3 jit_solution(2177770546129999280)
XLA Ops:
  8.0 12.7 %multiply_convert_fusion.3 = bf16[4,2,128,1024]{3,0,2,1:T(4,128)(2,1)S(1)} fusion(f32[128]{0:T(128)} %param.17, bf16[4,2,32,1]{2,1,0,3:T(2,128)(2,1)S(1)} %bitcast.385, bf16[4,8,128,1024]{3,2,1,0:T(8,128)(2,1)} %bitcast.388), kind=kOutput, calls=%fused_computation.55 | convolution fusion | flops 69206016 | bytes 10486784 | tf_op jit(solution)/shard_map/dot_general | solution.py:82
  20.8 5.4 constant_dynamic-slice_fusion.15
  39.5 14.1 %multiply_convert_fusion.2 = bf16[4,2,128,1024]{3,0,2,1:T(4,128)(2,1)} fusion(f32[128]{0:T(128)S(1)} %copy-done.35, bf16[4,2,32,1]{2,1,0,3:T(2,128)(2,1)S(1)} %bitcast.386, bf16[4,8,128,1024]{3,2,1,0:T(8,128)(2,1)} %bitcast.389), kind=kOutput, calls=%fused_computation.54 | convolution fusion | flops 69206016 | bytes 10486784 | tf_op jit(solution)/shard_map/dot_general | solution.py:82
  54.2 14.5 %multiply_convert_fusion.1 = bf16[4,2,128,1024]{3,0,2,1:T(4,128)(2,1)} fusion(f32[128]{0:T(128)S(1)} %copy-done.35, bf16[4,2,32,1]{2,1,0,3:T(2,128)(2,1)S(1)} %bitcast.387, bf16[4,8,128,1024]{3,2,1,0:T(8,128)(2,1)} %bitcast.390), kind=kOutput, calls=%fused_computation.53 | convolution fusion | flops 69206016 | bytes 10486784 | tf_op jit(solution)/shard_map/dot_general | solution.py:82
  72.6 7.4 %cosine_bitcast_fusion = (f32[4,512,128]{2,1,0:T(8,128)S(1)}, f32[4,512,128]{2,1,0:T(8,128)}) fusion(f32[512,4,128]{2,0,1:T(8,128)} %gather_fusion.2, pred[512]{0:T(512)(128)(4,1)S(1)} %compare_and_fusion), kind=kLoop, calls=%fused_computation.113 | loop fusion | flops 262144 | bytes 3146240 | tf_op jit(solution)/shard_map/cos | solution.py:76
  80.0 14.2 %multiply_convert_fusion = bf16[4,2,128,1024]{3,0,2,1:T(4,128)(2,1)} fusion(f32[128]{0:T(128)S(1)} %copy-done.35, bf16[4,2,32,1]{2,1,0,3:T(2,128)(2,1)S(1)} %bitcast.384, bf16[4,8,128,1024]{3,2,1,0:T(8,128)(2,1)} %bitcast.391), kind=kOutput, calls=%fused_computation.52 | convolution fusion | flops 69206016 | bytes 10486784 | tf_op jit(solution)/shard_map/dot_general | solution.py:82
  97.2 4.4 copy.24
  101.6 4.6 reshape.423
  106.2 4.7 fusion.100
  114.8 4.5 reshape.525
  119.3 8.3 %constant_dynamic-slice_fusion.11 = (bf16[1,2,128,1024]{3,0,2,1:T(2,128)(2,1)S(1)}, bf16[1,2,128,1024]{3,0,2,1:T(2,128)(2,1)S(1)}, bf16[1,2,128,1024]{3,0,2,1:T(2,128)(2,1)S(1)}, bf16[1,2,128,1024]{3,0,2,1:T(2,128)(2,1)S(1)}) fusion(bf16[4,2,128,1024]{3,0,2,1:T(4,128)(2,1)} %multiply_convert_fusion.2, s32[]{:T(128)S(6)} %select_n.160, s32[]{:T(128)S(6)} %select_n.166, ...), kind=kLoop, calls=%fused_computation.207 | loop fusion | bytes 4194320 | tf_op jit(solution)/shard_map/jit(dynamic_index_in_dim)/dynamic_slice | solution.py:87
  134.7 13.2 %all-reduce.5.cloned.1.call-done = bf16[1024,512]{1,0:T(8,128)(2,1)} async-done(((bf16[1024,512]{1,0:T(8,128)(2,1)}), bf16[1024,512]{1,0:T(8,128)(2,1)}) %all-reduce.5.cloned.1.call-update) | async-done | bytes 1048592 | tf_op jit(solution)/shard_map/psum | solution.py:100
  150.8 4.9 gather_fusion.3
  160.7 11.7 %collective-permute-done.4 = bf16[2,128,1024]{2,1,0:T(8,128)(2,1)} collective-permute-done((bf16[2,128,1024]{2,1,0:T(8,128)(2,1)}, bf16[2,128,1024]{2,1,0:T(8,128)(2,1)}, u32[]{:S(2)}, u32[]{:S(2)}) %collective-permute-start.4) | collective-permute-done | bytes 524320 | tf_op jit(solution)/shard_map/ppermute | solution.py:91
  172.4 5.8 collective-permute-done.5
  181.2 4.3 copy.27
  185.5 4.5 reshape.424
  190.0 4.8 fusion.101
  194.8 4.4 constant_dynamic-slice_fusion.7
  210.7 4.8 maximum_maximum_fusion
  215.5 29.8 %collective-permute-done.7 = bf16[2,128,1024]{2,1,0:T(8,128)(2,1)} collective-permute-done((bf16[2,128,1024]{2,1,0:T(8,128)(2,1)}, bf16[2,128,1024]{2,1,0:T(8,128)(2,1)}, u32[]{:S(2)}, u32[]{:S(2)}) %collective-permute-start.7) | collective-permute-done | bytes 524320 | tf_op jit(solution)/shard_map/ppermute | solution.py:91
  248.3 4.3 copy.30
  252.6 4.5 reshape.425
  257.1 9.0 %constant_dynamic-slice_fusion.3 = (bf16[1,2,128,1024]{3,0,2,1:T(2,128)(2,1)}, bf16[1,2,128,1024]{3,0,2,1:T(2,128)(2,1)S(1)}, bf16[1,2,128,1024]{3,0,2,1:T(2,128)(2,1)S(1)}, bf16[1,2,128,1024]{3,0,2,1:T(2,128)(2,1)S(1)}) fusion(bf16[4,2,128,1024]{3,0,2,1:T(4,128)(2,1)} %multiply_convert_fusion, s32[]{:T(128)S(6)} %select_n.160, s32[]{:T(128)S(6)} %select_n.166, ...), kind=kLoop, calls=%fused_computation.199 | loop fusion | bytes 4194320 | tf_op jit(solution)/shard_map/jit(dynamic_index_in_dim)/dynamic_slice | solution.py:87
  279.9 31.8 %collective-permute-done.10 = bf16[2,128,1024]{2,1,0:T(8,128)(2,1)} collective-permute-done((bf16[2,128,1024]{2,1,0:T(8,128)(2,1)}, bf16[2,128,1024]{2,1,0:T(8,128)(2,1)}, u32[]{:S(2)}, u32[]{:S(2)}) %collective-permute-start.10) | collective-permute-done | bytes 524320 | tf_op jit(solution)/shard_map/ppermute | solution.py:91
  311.7 5.0 collective-permute-done.11
  319.7 4.4 copy.33
  324.0 4.5 reshape.426
  328.5 4.7 fusion.103
  334.6 42.2 %while.76 = (s32[]{:T(128)}, f32[1,1024,128]{2,1,0:T(8,128)S(1)}, f32[1,1024,128]{2,1,0:T(8,128)}, f32[1,1024,128]{2,1,0:T(8,128)S(1)}, f32[1,1,1]{2,1,0:T(1,128...) while((s32[]{:T(128)}, f32[1,1024,128]{2,1,0:T(8,128)S(1)}, ...), condition=%wide.region_5.6_spmd.clone, body=%wide.region_4.5_spmd.clone.sunk | while | flops 806092800 | bytes 8388811 | solution.py:54
  334.8 5.1 multiply_add_fusion.8
  340.1 5.2 multiply_add_fusion.8
  345.3 5.1 multiply_add_fusion.8
  350.6 5.1 multiply_add_fusion.8
  355.9 5.1 multiply_add_fusion.8
  361.1 5.2 multiply_add_fusion.8
  366.5 5.1 multiply_add_fusion.8
  371.7 5.1 multiply_add_fusion.8
  376.8 4.5 reshape.528
  385.4 4.5 gather_fusion.5
  396.0 4.6 maximum_maximum_fusion.1
  400.6 35.4 %while.77 = (s32[]{:T(128)}, f32[1,1024,128]{2,1,0:T(8,128)S(1)}, f32[1,1024,128]{2,1,0:T(8,128)S(1)}, f32[1,1024,128]{2,1,0:T(8,128)S(1)}, f32[1,1,1]{2,1,0:T(1...) while((s32[]{:T(128)}, f32[1,1024,128]{2,1,0:T(8,128)S(1)}, ...), condition=%wide.region_12.13_spmd.clone, body=%wide.region_11.12_spmd.clone.sunk | while | flops 806092800 | bytes 8388811 | solution.py:54
  405.2 4.3 multiply_add_fusion.9
  409.6 4.3 multiply_add_fusion.9
  414.1 4.3 multiply_add_fusion.9
  418.5 4.3 multiply_add_fusion.9
  422.9 4.3 multiply_add_fusion.9
  427.4 4.3 multiply_add_fusion.9
  431.8 4.3 multiply_add_fusion.9
  436.1 4.5 reshape.531
  443.6 4.5 gather_fusion.7
  457.7 35.4 %while.78 = (s32[]{:T(128)}, f32[1,1024,128]{2,1,0:T(8,128)S(1)}, f32[1,1024,128]{2,1,0:T(8,128)S(1)}, f32[1,1024,128]{2,1,0:T(8,128)S(1)}, f32[1,1,1]{2,1,0:T(1...) while((s32[]{:T(128)}, f32[1,1024,128]{2,1,0:T(8,128)S(1)}, ...), condition=%wide.region_19.20_spmd.clone, body=%wide.region_18.19_spmd.clone.sunk | while | flops 806092800 | bytes 8388811 | solution.py:54
  462.3 4.3 multiply_add_fusion.10
  466.7 4.3 multiply_add_fusion.10
  471.2 4.3 multiply_add_fusion.10
  475.6 4.3 multiply_add_fusion.10
  480.0 4.3 multiply_add_fusion.10
  484.5 4.3 multiply_add_fusion.10
  488.9 4.3 multiply_add_fusion.10
  493.2 4.5 reshape.534
  501.9 4.5 gather_fusion.9
  515.8 35.4 %while.79 = (s32[]{:T(128)}, f32[1,1024,128]{2,1,0:T(8,128)S(1)}, f32[1,1024,128]{2,1,0:T(8,128)S(1)}, f32[1,1024,128]{2,1,0:T(8,128)S(1)}, f32[1,1,1]{2,1,0:T(1...) while((s32[]{:T(128)}, f32[1,1024,128]{2,1,0:T(8,128)S(1)}, ...), condition=%wide.region_26.27_spmd.clone, body=%wide.region_25.26_spmd.clone.sunk | while | flops 806092800 | bytes 8388811 | solution.py:54
  516.0 4.3 multiply_add_fusion.11
  579.1 37.9 %copy.34 = bf16[4,1024,2,512]{3,2,1,0:T(2,128)(2,1)} copy(bf16[4,1024,2,512]{3,1,2,0:T(8,128)(2,1)S(1)} %pad_maximum_fusion) | data formatting | bytes 16777216 | tf_op jit(solution)/shard_map/stack | solution.py:120
  (261 shorter events, 174.8 us)
Async XLA Ops:
  6.5 62.7 %copy-start = (f32[4,512,128]{2,1,0:T(8,128)S(1)}, f32[4,512,128]{2,1,0:T(8,128)}, u32[]{:S(2)}) copy-start(f32[4,512,128]{2,1,0:T(8,128)} %param.19) | copy-start | bytes 3145732
  6.5 141.4 %all-reduce.5.cloned.1.call-start = ((), (), s32[]{:S(2)}) async-start(), calls=%async_computation | async-start | bytes 2097152 | tf_op jit(solution)/shard_map/psum | solution.py:100
  27.1 67.1 %collective-permute-start = (bf16[2,128,1024]{2,1,0:T(8,128)(2,1)}, bf16[2,128,1024]{2,1,0:T(8,128)(2,1)}, u32[]{:S(2)}, u32[]{:S(2)}) collective-permute-start(bf16[2,128,1024]{2,1,0:T(8,128)(2,1)} %bitcast.333), channel_id=1, source_target_pairs={{0,4},{4,8},{8,12},{12,0},{1,5},{5,9},{9,13},{13,1},{2,6},{6,10},{... | collective-permute-start | bytes 1572872 | tf_op jit(solution)/shard_map/ppermute | solution.py:91
  28.4 6.8 %copy-start.2 = (s32[512]{0:T(512)S(1)}, s32[512]{0:T(512)}, u32[]{:S(2)}) copy-start(s32[512]{0:T(512)} %param.18) | copy-start | bytes 6148
  29.4 64.8 %collective-permute-start.1 = (bf16[2,128,1024]{2,1,0:T(8,128)(2,1)}, bf16[2,128,1024]{2,1,0:T(8,128)(2,1)}, u32[]{:S(2)}, u32[]{:S(2)}) collective-permute-start(bf16[2,128,1024]{2,1,0:T(8,128)(2,1)} %bitcast.332), channel_id=1, source_target_pairs={{0,8},{4,12},{8,0},{12,4},{1,9},{5,13},{9,1},{13,5},{2,10},{6,14},... | collective-permute-start | bytes 1572872 | tf_op jit(solution)/shard_map/ppermute | solution.py:91
  31.4 7.5 %copy-start.34 = (s32[8]{0:T(128)S(1)}, s32[8]{0:T(128)}, u32[]{:S(2)}) copy-start(s32[8]{0:T(128)} %constant.344) | copy-start | bytes 100
  31.4 8.1 %copy-start.35 = (f32[128]{0:T(128)S(1)}, f32[128]{0:T(128)}, u32[]{:S(2)}) copy-start(f32[128]{0:T(128)} %param.17) | copy-start | bytes 1540
  31.4 62.8 %collective-permute-start.2 = (bf16[2,128,1024]{2,1,0:T(8,128)(2,1)}, bf16[2,128,1024]{2,1,0:T(8,128)(2,1)}, u32[]{:S(2)}, u32[]{:S(2)}) collective-permute-start(bf16[2,128,1024]{2,1,0:T(8,128)(2,1)} %bitcast.331), channel_id=1, source_target_pairs={{0,12},{4,0},{8,4},{12,8},{1,13},{5,1},{9,5},{13,9},{2,14},{6,2},{... | collective-permute-start | bytes 1572872 | tf_op jit(solution)/shard_map/ppermute | solution.py:91
  39.5 14.1 %copy-start.33 = (s32[8]{0:T(128)S(1)}, s32[8]{0:T(128)}, u32[]{:S(2)}) copy-start(s32[8]{0:T(128)} %constant.345) | copy-start | bytes 100
  54.2 14.5 %copy-start.32 = (s32[8]{0:T(128)S(1)}, s32[8]{0:T(128)}, u32[]{:S(2)}) copy-start(s32[8]{0:T(128)} %constant.346) | copy-start | bytes 100
  80.0 14.2 %copy-start.27 = (bf16[1,2,128,1024]{3,2,0,1:T(8,128)(2,1)S(1)}, bf16[1,2,128,1024]{3,2,0,1:T(8,128)(2,1)}, u32[]{:S(2)}) copy-start(bf16[1,2,128,1024]{3,2,0,1:T(8,128)(2,1)} %copy.137) | copy-start | bytes 1572868
  112.3 165.2 %all-reduce.7.cloned.1.call-start = ((), (), s32[]{:S(2)}) async-start(), calls=%async_computation.2 | async-start | bytes 2097152 | tf_op jit(solution)/shard_map/psum | solution.py:100
  128.6 32.1 %collective-permute-start.3 = (bf16[2,128,1024]{2,1,0:T(8,128)(2,1)}, bf16[2,128,1024]{2,1,0:T(8,128)(2,1)}, u32[]{:S(2)}, u32[]{:S(2)}) collective-permute-start(bf16[2,128,1024]{2,1,0:T(8,128)(2,1)} %bitcast.329), channel_id=1, source_target_pairs={{0,4},{4,8},{8,12},{12,0},{1,5},{5,9},{9,13},{13,1},{2,6},{6,10},{... | collective-permute-start | bytes 1572872 | tf_op jit(solution)/shard_map/ppermute | solution.py:91
  129.6 42.8 %collective-permute-start.4 = (bf16[2,128,1024]{2,1,0:T(8,128)(2,1)}, bf16[2,128,1024]{2,1,0:T(8,128)(2,1)}, u32[]{:S(2)}, u32[]{:S(2)}) collective-permute-start(bf16[2,128,1024]{2,1,0:T(8,128)(2,1)} %bitcast.328), channel_id=1, source_target_pairs={{0,8},{4,12},{8,0},{12,4},{1,9},{5,13},{9,1},{13,5},{2,10},{6,14},... | collective-permute-start | bytes 1572872 | tf_op jit(solution)/shard_map/ppermute | solution.py:91
  133.8 44.5 %collective-permute-start.5 = (bf16[2,128,1024]{2,1,0:T(8,128)(2,1)}, bf16[2,128,1024]{2,1,0:T(8,128)(2,1)}, u32[]{:S(2)}, u32[]{:S(2)}) collective-permute-start(bf16[2,128,1024]{2,1,0:T(8,128)(2,1)} %bitcast.327), channel_id=1, source_target_pairs={{0,12},{4,0},{8,4},{12,8},{1,13},{5,1},{9,5},{13,9},{2,14},{6,2},{... | collective-permute-start | bytes 1572872 | tf_op jit(solution)/shard_map/ppermute | solution.py:91
  149.4 1.4 copy-start.4
  156.9 21.3 %copy-start.28 = (bf16[1,2,128,1024]{3,2,0,1:T(8,128)(2,1)S(1)}, bf16[1,2,128,1024]{3,2,0,1:T(8,128)(2,1)}, u32[]{:S(2)}) copy-start(bf16[1,2,128,1024]{3,2,0,1:T(8,128)(2,1)} %copy.133) | copy-start | bytes 1572868
  190.0 4.8 copy-start.7
  200.2 15.3 %collective-permute-start.6 = (bf16[2,128,1024]{2,1,0:T(8,128)(2,1)}, bf16[2,128,1024]{2,1,0:T(8,128)(2,1)}, u32[]{:S(2)}, u32[]{:S(2)}) collective-permute-start(bf16[2,128,1024]{2,1,0:T(8,128)(2,1)} %bitcast.325), channel_id=1, source_target_pairs={{0,4},{4,8},{8,12},{12,0},{1,5},{5,9},{9,13},{13,1},{2,6},{6,10},{... | collective-permute-start | bytes 1572872 | tf_op jit(solution)/shard_map/ppermute | solution.py:91
  201.2 44.1 %collective-permute-start.7 = (bf16[2,128,1024]{2,1,0:T(8,128)(2,1)}, bf16[2,128,1024]{2,1,0:T(8,128)(2,1)}, u32[]{:S(2)}, u32[]{:S(2)}) collective-permute-start(bf16[2,128,1024]{2,1,0:T(8,128)(2,1)} %bitcast.324), channel_id=1, source_target_pairs={{0,8},{4,12},{8,0},{12,4},{1,9},{5,13},{9,1},{13,5},{2,10},{6,14},... | collective-permute-start | bytes 1572872 | tf_op jit(solution)/shard_map/ppermute | solution.py:91
  202.2 43.1 %collective-permute-start.8 = (bf16[2,128,1024]{2,1,0:T(8,128)(2,1)}, bf16[2,128,1024]{2,1,0:T(8,128)(2,1)}, u32[]{:S(2)}, u32[]{:S(2)}) collective-permute-start(bf16[2,128,1024]{2,1,0:T(8,128)(2,1)} %bitcast.323), channel_id=1, source_target_pairs={{0,12},{4,0},{8,4},{12,8},{1,13},{5,1},{9,5},{13,9},{2,14},{6,2},{... | collective-permute-start | bytes 1572872 | tf_op jit(solution)/shard_map/ppermute | solution.py:91
  208.6 126.0 %all-reduce.9.cloned.1.call-start = ((), (), s32[]{:S(2)}) async-start(), calls=%async_computation.4 | async-start | bytes 2097152 | tf_op jit(solution)/shard_map/psum | solution.py:100
  266.1 7.6 %copy-start.26 = (bf16[1024,1024]{0,1:T(8,128)(2,1)S(1)}, bf16[1024,1024]{0,1:T(8,128)(2,1)}, u32[]{:S(2)}) copy-start(bf16[1024,1024]{0,1:T(8,128)(2,1)} %reshape.425) | copy-start | bytes 6291460
  267.0 12.9 %collective-permute-start.9 = (bf16[2,128,1024]{2,1,0:T(8,128)(2,1)}, bf16[2,128,1024]{2,1,0:T(8,128)(2,1)}, u32[]{:S(2)}, u32[]{:S(2)}) collective-permute-start(bf16[2,128,1024]{2,1,0:T(8,128)(2,1)} %bitcast.321), channel_id=1, source_target_pairs={{0,4},{4,8},{8,12},{12,0},{1,5},{5,9},{9,13},{13,1},{2,6},{6,10},{... | collective-permute-start | bytes 1572872 | tf_op jit(solution)/shard_map/ppermute | solution.py:91
  268.2 43.6 %collective-permute-start.10 = (bf16[2,128,1024]{2,1,0:T(8,128)(2,1)}, bf16[2,128,1024]{2,1,0:T(8,128)(2,1)}, u32[]{:S(2)}, u32[]{:S(2)}) collective-permute-start(bf16[2,128,1024]{2,1,0:T(8,128)(2,1)} %bitcast.320), channel_id=1, source_target_pairs={{0,8},{4,12},{8,0},{12,4},{1,9},{5,13},{9,1},{13,5},{2,10},{6,14},... | collective-permute-start | bytes 1572872 | tf_op jit(solution)/shard_map/ppermute | solution.py:91
  272.3 44.5 %collective-permute-start.11 = (bf16[2,128,1024]{2,1,0:T(8,128)(2,1)}, bf16[2,128,1024]{2,1,0:T(8,128)(2,1)}, u32[]{:S(2)}, u32[]{:S(2)}) collective-permute-start(bf16[2,128,1024]{2,1,0:T(8,128)(2,1)} %bitcast.319), channel_id=1, source_target_pairs={{0,12},{4,0},{8,4},{12,8},{1,13},{5,1},{9,5},{13,9},{2,14},{6,2},{... | collective-permute-start | bytes 1572872 | tf_op jit(solution)/shard_map/ppermute | solution.py:91
  277.6 221.4 %all-reduce.11.cloned.1.call-start = ((), (), s32[]{:S(2)}) async-start(), calls=%async_computation.6 | async-start | bytes 2097152 | tf_op jit(solution)/shard_map/psum | solution.py:100
  334.6 217.7 %all-gather.5.cloned.1.call-start = ((), (), s32[]{:S(2)}) async-start(), calls=%async_computation.1 | async-start | bytes 1310720 | tf_op jit(solution)/shard_map/all_gather | solution.py:108
  376.8 4.5 copy-start.20
  376.8 4.5 copy-start.21
  382.3 175.5 %all-gather.7.cloned.1.call-start = ((), (), s32[]{:S(2)}) async-start(), calls=%async_computation.3 | async-start | bytes 1310720 | tf_op jit(solution)/shard_map/all_gather | solution.py:108
  384.0 1.3 copy-start.5
  395.9 4.6 copy-start.16
  395.9 4.6 copy-start.18
  436.1 4.5 copy-start.17
  436.1 4.5 copy-start.19
  440.6 1.3 copy-start.31
  441.5 123.2 %all-gather.9.cloned.1.call-start = ((), (), s32[]{:S(2)}) async-start(), calls=%async_computation.5 | async-start | bytes 1310720 | tf_op jit(solution)/shard_map/all_gather | solution.py:108
  442.2 1.3 copy-start.6
  453.8 3.9 copy-start.12
  453.8 3.8 copy-start.14
  493.2 4.6 copy-start.13
  493.2 4.6 copy-start.15
  498.7 73.8 %all-gather.11.cloned.1.call-start = ((), (), s32[]{:S(2)}) async-start(), calls=%async_computation.7 | async-start | bytes 1310720 | tf_op jit(solution)/shard_map/all_gather | solution.py:108
  500.5 1.3 copy-start.3
  511.9 3.8 copy-start.11
  552.3 1.5 copy-start.8
  553.9 1.6 copy-start.22
  557.8 1.6 copy-start.9
  559.5 1.6 copy-start.23
  567.2 1.6 copy-start.24
  572.4 1.5 copy-start.10
  574.0 1.6 copy-start.25
  575.6 2.3 copy-start.29
  575.6 2.3 copy-start.30
  579.1 37.9 %copy-start.1 = (f32[4,512,128]{2,1,0:T(8,128)S(1)}, f32[4,512,128]{2,1,0:T(8,128)}, u32[]{:S(2)}) copy-start(f32[4,512,128]{2,1,0:T(8,128)} %param.19) | copy-start | bytes 3145732
Sparse Core Ops, SparseCore 0:
  112.5 35.3 all-reduce.4
  208.7 37.1 all-reduce.6
  277.7 35.5 all-reduce.8
  334.7 34.3 all-reduce.10
  382.4 15.2 all-gather.4
  441.7 15.2 all-gather.6
  498.8 15.2 all-gather.8
  552.4 15.2 all-gather.10

commit v4 on v2

--- a/solution.py
+++ b/solution.py
@@ -52,7 +52,7 @@
         dirn = rho_next * rho * dirn + 2.0 * rho_next / radius * res
         return sol, res, dirn, rho_next
 
-    sol, _, _, _ = lax.fori_loop(0, ITERS, body, (sol, res, dirn, rho))
+    sol, _, _, _ = lax.fori_loop(0, ITERS, body, (sol, res, dirn, rho), unroll=True)
     response = jnp.sum(steer * sol, axis=1, keepdims=True)
     weights = (sol / response).astype(jnp.bfloat16)
     return weights.reshape(weights.shape[0], 2, stations, weights.shape[2])

time: 491 us -> 446 us (0.908); the launches traced: 490 us -> 437 us
  local copies, waits for them, and re-layouts: 73.7 us -> 48.4 us
  matrix products: 105 us -> 83.7 us
  other arithmetic: 40.3 us -> 23.3 us
  waiting for transfers between devices: 60.4 us -> 70.3 us
    while x24 -> x0, local copies, waits for them, and re-layouts: 22.5 us -> none
    dot_general x8 -> x7, matrix products: 55.4 us -> 33.9 us  [body(): img = jnp.einsum('cjk,ckb->cjb', block, dirn, precision=high)]
    concatenate x3 -> x0, other arithmetic: 11.4 us -> none  [the longest x2 7.09 us: chebyshev(): steer = jnp.concatenate((steer_real, steer_imag), axis=1)]
    reduce_scatter x1, waiting for transfers between devices: 25.7 us -> 35.6 us  [local(): lax.psum_scatter(part, 'tm', scatter_dimension=0, tiled=True)]
  transfers between devices with their start and end apart: 5 -> 5, of which waited for: 2 -> 2; matrix products, arithmetic and copies ran while one was open for 7% -> 6% of each run, Pallas kernels for 0% -> 0%
where the time goes in v4:
time: 446 us; the launch traced here: 437 us
  blocking collectives  191 us (43%)
  matrix products  83.7 us (19%)
  waiting for transfers between devices  70.3 us (16%)
  local copies, waits for them, and re-layouts  48.4 us (11%)
  other arithmetic  23.3 us (5%)
  between operations  16 us (4%)
  starting transfers between devices  4.5 us (1%)
    all_to_all x1, blocking collectives, local(): lax.all_to_all(spectra, 'chan', split_axis=0, concat_axis=2, tiled=True)  191 us
    reduce_scatter x1, waiting for transfers between devices, local(): lax.psum_scatter(part, 'tm', scatter_dimension=0, tiled=True)  35.6 us
    all_gather x1, waiting for transfers between devices, local(): weights = lax.all_gather(weights, 'tm', axis=0, tiled=True)  34.6 us
    dot_general x7, matrix products, body(): img = jnp.einsum('cjk,ckb->cjb', block, dirn, precision=high)  33.9 us
    dot_general x1, matrix products, local(): jnp.dot(dft_table(count), samples.reshape(2 * count, -1), preferred_eleme...  17.8 us
    dot_general x1, matrix products, local(): jnp.einsum('cat,cbt->cab', stacked, stacked, preferred_element_type=jnp.f...  16.9 us
    convert_element_type x1, local copies, waits for them, and re-layouts, local(): return formed.astype(jnp.bfloat16)  16.4 us
    dot_general x1, matrix products, local(): jnp.einsum('cat,cakb->ctkb', stacked, weight_cat, preferred_element_type=...  15.1 us
  transfers between devices with their start and end apart: 5, of which 2 were waited for; matrix products, arithmetic and copies ran while one was open for 6% of the time, Pallas kernels for 0%

profile of v4, /device:TPU:0, one launch (start us, length us, event | category | flops | bytes accessed | tf_op | source)
XLA Modules:
  0.0 436.7 jit_solution(17251020101844814980)
XLA Ops:
  6.5 0.0 copy-start.6
  6.5 0.0 reduce-scatter.2.cloned.1.call-start
  6.5 1.3 dynamic-slice_bitcast_fusion
  7.8 0.5 collective-permute-start
  8.3 2.6 collective-permute-start.1
  10.9 1.4 collective-permute-start.2
  12.3 0.1 negate_convert_fusion
  12.3 0.1 fusion.33
  12.4 0.1 maximum_maximum_fusion
  12.5 0.0 copy-done.6
  12.5 17.8 %multiply_convert_fusion = bf16[16,2,128,1024]{3,0,2,1:T(8,128)(2,1)} fusion(f32[128]{0:T(128)S(1)} %copy-done.6, bf16[16,2,32,1]{2,0,3,1:T(8,128)(2,1)S(1)} %bitcast.119, bf16[4,8,128,1024]{3,2,1,0:T(8,128)(2,1)} %bitcast.120), kind=kOutput, calls=%fused_computation.3 | convolution fusion | flops 276824064 | bytes 16779776 | tf_op jit(solution)/shard_map/dot_general | solution.py:83
  30.3 0.0 collective-permute-done
  30.3 0.0 collective-permute-done.1
  30.3 0.0 collective-permute-done.2
  30.3 0.1 maximum_bitcast_fusion.3
  30.4 0.6 gather_fusion
  31.0 0.2 copy_bitcast_fusion
  31.2 11.3 %copy.20 = bf16[16,2,128,1024]{3,2,1,0:T(8,128)(2,1)} copy(bf16[16,2,128,1024]{3,0,2,1:T(8,128)(2,1)} %multiply_convert_fusion) | data formatting | bytes 16777216 | tf_op jit(solution)/shard_map/optimization_barrier | solution.py:91
  42.5 190.5 %all_to_all.15 = bf16[16,2,128,1024]{3,2,1,0:T(8,128)(2,1)} all-to-all(bf16[16,2,128,1024]{3,2,1,0:T(8,128)(2,1)} %copy.20), channel_id=1, replica_groups=mesh['groups'=2,'chan'=4,'tm'=4] {'chan'}, dimensions={0} | all-to-all | bytes 16777216 | tf_op jit(solution)/shard_map/all_to_all | solution.py:94
  233.1 8.4 %copy.21 = bf16[4,4,2,128,1024]{4,3,0,2,1:T(8,128)(2,1)} copy(bf16[4,4,2,128,1024]{4,3,2,1,0:T(8,128)(2,1)} %bitcast.112) | data formatting | bytes 16777216 | tf_op jit(solution)/shard_map/all_to_all | solution.py:94
  241.4 16.9 %fusion.42 = f32[4,1024,1024]{2,1,0:T(8,128)} fusion(bf16[4,1024,1024]{2,1,0:T(8,128)(2,1)} %bitcast.113), kind=kOutput, calls=%fused_computation.101 | convolution fusion | flops 8589934592 | bytes 25165824 | tf_op jit(solution)/shard_map/cat,cbt->cab/dot_general | solution.py:99
  258.4 6.7 %fusion.10 = (bf16[4,512,512]{2,1,0:T(8,128)(2,1)S(1)}, bf16[4,512,512]{2,1,0:T(8,128)(2,1)S(1)}) fusion(f32[4,1024,1024]{2,1,0:T(8,128)} %fusion.42), kind=kLoop, calls=%fused_computation.15 | loop fusion | flops 4194304 | bytes 20971520 | tf_op jit(solution)/shard_map/convert
  265.1 2.2 pad_maximum_fusion
  267.3 0.0 copy-start.5
  267.3 0.0 reduce-scatter.2.cloned.1.call-update
  267.3 0.0 all-gather.2.cloned.1.call-start
  267.4 0.6 copy-done.5
  268.0 1.6 gather_fusion.1
  269.6 5.6 %select_cosine_fusion = (f32[512,512]{1,0:T(8,128)}, f32[512,512]{1,0:T(8,128)}) fusion(f32[512,512]{1,0:T(8,128)S(1)} %gather_fusion.1, pred[512]{0:T(512)(128)(4,1)S(1)} %compare_and_fusion), kind=kLoop, calls=%fused_computation.60 | loop fusion | flops 262144 | bytes 3146240 | tf_op jit(solution)/shard_map/cos | solution.py:110
  275.3 35.6 %reduce-scatter.2.cloned.1.call-done = bf16[1,1024,512]{2,1,0:T(8,128)(2,1)} async-done(((bf16[4,1024,512]{2,1,0:T(8,128)(2,1)}), bf16[1,1024,512]{2,1,0:T(8,128)(2,1)}) %reduce-scatter.2.cloned.1.call-update) | async-done | bytes 1048592 | tf_op jit(solution)/shard_map/reduce_scatter | solution.py:104
  310.8 1.5 convert_multiply_fusion
  312.4 0.1 slice_bitcast_fusion.2
  312.4 4.7 %gather_fusion.2 = f32[512]{0:T(512)S(1)} fusion(f32[512,512]{1,0:T(8,128)S(1)} %slice_bitcast_fusion.2, s32[512]{0:T(512)S(1)} %bitcast.111), kind=kCustom, calls=%fused_computation.2 | custom fusion | bytes 8192 | tf_op jit(solution)/shard_map/jit(diagonal)/gather | solution.py:26
  317.1 0.6 reduce.6
  318.4 1.8 sqrt_reduce_fusion
  320.2 0.6 reduce_max.11
  322.1 0.0 copy-start.1
  322.1 0.0 copy-start.2
  322.1 0.0 copy-start.3
  322.1 0.0 copy-start.4
  322.1 6.8 %convolution_subtract_fusion.4 = f32[1024,512]{1,0:T(8,128)S(1)} fusion(f32[512,512]{1,0:T(8,128)} %get-tuple-element.20, f32[512,512]{1,0:T(8,128)} %get-tuple-element.19, f32[1,512,512]{2,1,0:T(8,128)} %get-tuple-element.17, f32[1,512,512]{2,1,0:T(8,128)} %get-tuple-element.18, f32[1,512,512]{2,1,0:T(8,128)S(1)} %get-tuple-element.16, f32[]{:T(128)} %bitcast.24), kind=kOutput, calls=%fused_computation.40 | convolution fusion | flops 3226468352 | bytes 7340036 | tf_op jit(solution)/shard_map/eval_jaxpr/cjk,ckb->cjb/dot_general | solution.py:49
  328.9 0.0 copy-start.7
  328.9 0.0 copy-done.1
  328.9 0.0 copy-done.2
  328.9 0.0 copy-done.3
  328.9 0.0 copy-done.4
  328.9 3.6 convolution_subtract_fusion.3
  332.6 0.0 copy-start.8
  332.6 0.0 copy-done.7
  332.6 4.3 multiply_add_fusion.3
  336.9 0.0 copy-done.8
  336.9 3.8 convolution_subtract_fusion.1
  340.7 3.5 convolution_subtract_fusion
  344.2 3.6 fusion.13
  347.8 8.3 %multiply_reduce_fusion = (f32[512]{0:T(512)S(1)}, f32[1024,512]{1,0:T(8,128)S(1)}) fusion(f32[512,512]{1,0:T(8,128)S(1)} %copy-done.4, f32[512,512]{1,0:T(8,128)S(1)} %copy-done.3, f32[1024,512]{1,0:T(8,128)S(1)} %convolution_subtract_fusion, f32[1024,512]{1,0:T(8,128)S(1)} %fusion.13, f32[]{:T(128)} %bitcast.39, f32[]{:T(128)} %bitcast.38, f32[]{:T(128)} %bitcast.37, ...), kind=kOutput, calls=%fused_computation.24 | convolution fusion | flops 3245866496 | bytes 19925044 | tf_op jit(solution)/shard_map/eval_jaxpr/cjk,ckb->cjb/dot_general | solution.py:49
  356.1 1.3 divide_convert_fusion
  357.4 0.0 all-gather.2.cloned.1.call-update
  357.4 34.6 %all-gather.2.cloned.1.call-done = bf16[4,2,512,512]{3,2,0,1:T(8,128)(2,1)} async-done(((bf16[1,2,512,512]{3,2,0,1:T(8,128)(2,1)}), bf16[4,2,512,512]{3,2,0,1:T(8,128)(2,1)}) %all-gather.2.cloned.1.call-update) | async-done | bytes 4194320 | tf_op jit(solution)/shard_map/all_gather | solution.py:113
  392.0 2.7 slice_bitcast_fusion
  394.7 0.8 copy-done
  395.5 0.1 fusion.38
  395.6 2.3 maximum_bitcast_fusion.1
  397.9 15.1 %fusion.6 = bf16[4,1024,2,512]{3,1,2,0:T(8,128)(2,1)} fusion(bf16[4,1024,1024,1]{2,1,3,0:T(8,128)(2,1)} %bitcast.114, bf16[4,1024,1,512]{3,1,2,0:T(8,128)(2,1)} %get-tuple-element.14, bf16[4,1024,1,512]{3,1,2,0:T(8,128)(2,1)S(1)} %get-tuple-element.13), kind=kOutput, calls=%fused_computation.11 | convolution fusion | flops 8610906112 | bytes 25165824 | tf_op jit(solution)/shard_map/cat,cakb->ctkb/dot_general | solution.py:125
  413.0 16.4 %copy.25 = bf16[4,1024,2,512]{3,2,1,0:T(2,128)(2,1)} copy(bf16[4,1024,2,512]{3,1,2,0:T(8,128)(2,1)} %fusion.6) | data formatting | bytes 16777216 | tf_op jit(solution)/shard_map/convert_element_type | solution.py:126
  (8 shorter events, 0.1 us)
Async XLA Ops:
  6.5 5.9 %copy-start.6 = (f32[128]{0:T(128)S(1)}, f32[128]{0:T(128)}, u32[]{:S(2)}) copy-start(f32[128]{0:T(128)} %param.5) | copy-start | bytes 1540
  6.5 304.3 %reduce-scatter.2.cloned.1.call-start = ((), (), s32[]{:S(2)}) async-start(), calls=%async_computation.2 | async-start | bytes 5242880 | tf_op jit(solution)/shard_map/reduce_scatter | solution.py:104
  7.8 22.5 %collective-permute-start = (f32[1,512,128]{2,1,0:T(8,128)S(1)}, f32[1,512,128]{2,1,0:T(8,128)S(1)}, u32[]{:S(2)}, u32[]{:S(2)}) collective-permute-start(f32[1,512,128]{2,1,0:T(8,128)S(1)} %get-tuple-element.22), channel_id=1, source_target_pairs={{0,1},{1,2},{2,3},{3,0},{4,5},{5,6},{6,7},{7,4},{8,9},{9,10},{10,1... | collective-permute-start | bytes 786440 | tf_op jit(solution)/shard_map/ppermute | solution.py:70
  8.3 22.0 %collective-permute-start.1 = (f32[1,512,128]{2,1,0:T(8,128)S(1)}, f32[1,512,128]{2,1,0:T(8,128)S(1)}, u32[]{:S(2)}, u32[]{:S(2)}) collective-permute-start(f32[1,512,128]{2,1,0:T(8,128)S(1)} %get-tuple-element.24), channel_id=1, source_target_pairs={{0,2},{1,3},{2,0},{3,1},{4,6},{5,7},{6,4},{7,5},{8,10},{9,11},{10,... | collective-permute-start | bytes 786440 | tf_op jit(solution)/shard_map/ppermute | solution.py:70
  10.9 19.4 %collective-permute-start.2 = (f32[1,512,128]{2,1,0:T(8,128)S(1)}, f32[1,512,128]{2,1,0:T(8,128)S(1)}, u32[]{:S(2)}, u32[]{:S(2)}) collective-permute-start(f32[1,512,128]{2,1,0:T(8,128)S(1)} %get-tuple-element.23), channel_id=1, source_target_pairs={{0,3},{1,0},{2,1},{3,2},{4,7},{5,4},{6,5},{7,6},{8,11},{9,8},{10,9... | collective-permute-start | bytes 786440 | tf_op jit(solution)/shard_map/ppermute | solution.py:70
  267.3 0.7 copy-start.5
  267.3 124.7 %all-gather.2.cloned.1.call-start = ((), (), s32[]{:S(2)}) async-start(), calls=%async_computation.3 | async-start | bytes 5242880 | tf_op jit(solution)/shard_map/all_gather | solution.py:113
  322.1 6.8 %copy-start.1 = (f32[1,512,512]{2,1,0:T(8,128)S(1)}, f32[1,512,512]{2,1,0:T(8,128)}, u32[]{:S(2)}) copy-start(f32[1,512,512]{2,1,0:T(8,128)} %get-tuple-element.17) | copy-start | bytes 3145732
  322.1 6.8 %copy-start.2 = (f32[1,512,512]{2,1,0:T(8,128)S(1)}, f32[1,512,512]{2,1,0:T(8,128)}, u32[]{:S(2)}) copy-start(f32[1,512,512]{2,1,0:T(8,128)} %get-tuple-element.18) | copy-start | bytes 3145732
  322.1 6.8 %copy-start.3 = (f32[512,512]{1,0:T(8,128)S(1)}, f32[512,512]{1,0:T(8,128)}, u32[]{:S(2)}) copy-start(f32[512,512]{1,0:T(8,128)} %get-tuple-element.19) | copy-start | bytes 3145732
  322.1 6.8 %copy-start.4 = (f32[512,512]{1,0:T(8,128)S(1)}, f32[512,512]{1,0:T(8,128)}, u32[]{:S(2)}) copy-start(f32[512,512]{1,0:T(8,128)} %get-tuple-element.20) | copy-start | bytes 3145732
  328.9 3.7 copy-start.7
  332.6 4.3 copy-start.8
  392.0 3.4 copy-start
Sparse Core Ops, SparseCore 0:
  267.5 43.3 reduce-scatter.1
  357.5 34.4 all-gather.1

commit v5 on v4

--- a/solution.py
+++ b/solution.py
@@ -6,6 +6,7 @@
 from jax.sharding import PartitionSpec as P
 
 ITERS = 8
+TIME_PIECES = 2
 
 
 def dft_table(count):
@@ -80,23 +81,34 @@
     spec_count = samples.shape[3]
     chan_size = lax.axis_size("chan")
     tm_size = lax.axis_size("tm")
-    channelized = jnp.dot(
-        dft_table(count), samples.reshape(2 * count, -1), preferred_element_type=jnp.float32
-    )
-    channelized = channelized.reshape(count, 2, row_count, spec_count)
-    spectra = (channelized * station_gain[None, None, :, None]).astype(jnp.bfloat16)
     split_channels = (count // chan_size) % tm_size == 0
     if split_channels:
         phase = exchange_phase(steer_phase, tm_size)
-        spectra, phase = lax.optimization_barrier((spectra, phase))
     else:
         phase = steer_phase
-    owned = lax.all_to_all(spectra, "chan", split_axis=0, concat_axis=2, tiled=True)
+    table = dft_table(count)
+    pieces = TIME_PIECES if spec_count % TIME_PIECES == 0 else 1
+    width = spec_count // pieces
+    owned_pieces = []
+    for piece in range(pieces):
+        chunk = samples[:, :, :, piece * width : (piece + 1) * width]
+        channelized = jnp.dot(table, chunk.reshape(2 * count, -1), preferred_element_type=jnp.float32)
+        channelized = channelized.reshape(count, 2, row_count, width)
+        spectra = (channelized * station_gain[None, None, :, None]).astype(jnp.bfloat16)
+        if split_channels and piece == 0:
+            spectra, phase = lax.optimization_barrier((spectra, phase))
+        owned_pieces.append(
+            lax.all_to_all(spectra, "chan", split_axis=0, concat_axis=2, tiled=True)
+        )
+    owned = owned_pieces[0]
     chans = owned.shape[0]
     stations = owned.shape[2]
-    stacked = owned.reshape(chans, 2 * stations, spec_count)
+    stacked_pieces = [piece.reshape(chans, 2 * stations, width) for piece in owned_pieces]
     spectra_total = spec_count * tm_size
-    gram_sum = jnp.einsum("cat,cbt->cab", stacked, stacked, preferred_element_type=jnp.float32)
+    gram_sum = None
+    for stacked in stacked_pieces:
+        gram = jnp.einsum("cat,cbt->cab", stacked, stacked, preferred_element_type=jnp.float32)
+        gram_sum = gram if gram_sum is None else gram_sum + gram
     part_real = gram_sum[:, :stations, :stations] + gram_sum[:, stations:, stations:]
     part_imag = gram_sum[:, stations:, :stations] - gram_sum[:, :stations, stations:]
     part = jnp.concatenate((part_real, part_imag), axis=1).astype(jnp.bfloat16)
@@ -122,8 +134,11 @@
         ),
         axis=2,
     )
-    formed = jnp.einsum("cat,cakb->ctkb", stacked, weight_cat, preferred_element_type=jnp.float32)
-    return formed.astype(jnp.bfloat16)
+    formed = [
+        jnp.einsum("cat,cakb->ctkb", stacked, weight_cat, preferred_element_type=jnp.float32)
+        for stacked in stacked_pieces
+    ]
+    return jnp.concatenate(formed, axis=1).astype(jnp.bfloat16)
 
 
 def solution(mesh):

time: 446 us -> 452 us (1.013)
  blocking collectives: 191 us -> 0 us
  waiting for transfers between devices: 70.3 us -> 234 us
  matrix products: 83.7 us -> 94.5 us
  starting transfers between devices: 4.5 us -> 14.6 us
  other arithmetic: 23.3 us -> 32.3 us
    all_to_all x1 -> x0, blocking collectives: 191 us -> none  [local(): lax.all_to_all(spectra, 'chan', split_axis=0, concat_axis=2, tiled=True)]
    all_to_all x0 -> x2, waiting for transfers between devices: none -> 161 us  [local(): lax.all_to_all(spectra, 'chan', split_axis=0, concat_axis=2, tiled=True)]
    concatenate x0 -> x1, local copies, waits for them, and re-layouts: none -> 16.4 us  [local(): return jnp.concatenate(formed, axis=1).astype(jnp.bfloat16)]
    convert_element_type x1, local copies, waits for them, and re-layouts: 16.4 us -> 4.39 us  [local(): (channelized * station_gain[None, None, :, None]).astype(jnp.bfloat16)]
    all_to_all x0 -> x2, starting transfers between devices: none -> 11.5 us  [local(): lax.all_to_all(spectra, 'chan', split_axis=0, concat_axis=2, tiled=True)]
    dot_general x1 -> x2, matrix products: 16.9 us -> 26.6 us  [local(): jnp.einsum('cat,cbt->cab', stacked, stacked, preferred_element_type=jnp.f...]
    concatenate x0 -> x1, other arithmetic: none -> 7.25 us  [local(): return jnp.concatenate(formed, axis=1).astype(jnp.bfloat16)]
    slice x0 -> x1, local copies, waits for them, and re-layouts: none -> 5.27 us  [local(): chunk = samples[:, :, :, piece * width:(piece + 1) * width]]
  transfers between devices with their start and end apart: 5 -> 7, of which waited for: 2 -> 5; matrix products, arithmetic and copies ran while one was open for 6% -> 6% of each run, Pallas kernels for 0% -> 0%
where the time goes in v5:
time: 452 us; the launch traced here: 443 us
  waiting for transfers between devices  234 us (52%)
  matrix products  94.5 us (21%)
  local copies, waits for them, and re-layouts  51.4 us (11%)
  other arithmetic  32.3 us (7%)
  between operations  16.1 us (4%)
  starting transfers between devices  14.6 us (3%)
    all_to_all x2, waiting for transfers between devices, local(): lax.all_to_all(spectra, 'chan', split_axis=0, concat_axis=2, tiled=True)  161 us
    reduce_scatter x1, waiting for transfers between devices, local(): lax.psum_scatter(part, 'tm', scatter_dimension=0, tiled=True)  36 us
    all_gather x1, waiting for transfers between devices, local(): weights = lax.all_gather(weights, 'tm', axis=0, tiled=True)  34.6 us
    dot_general x7, matrix products, body(): img = jnp.einsum('cjk,ckb->cjb', block, dirn, precision=high)  33.8 us
    dot_general x2, matrix products, local(): jnp.einsum('cat,cbt->cab', stacked, stacked, preferred_element_type=jnp.f...  26.6 us
    dot_general x2, matrix products, local(): jnp.einsum('cat,cakb->ctkb', stacked, weight_cat, preferred_element_type=...  20.3 us
    concatenate x1, local copies, waits for them, and re-layouts, local(): return jnp.concatenate(formed, axis=1).astype(jnp.bfloat16)  16.4 us
    dot_general x2, matrix products, local(): jnp.dot(table, chunk.reshape(2 * count, -1), preferred_element_type=jnp.f...  13.7 us
  transfers between devices with their start and end apart: 7, of which 5 were waited for; matrix products, arithmetic and copies ran while one was open for 6% of the time, Pallas kernels for 0%

profile of v5, /device:TPU:0, one launch (start us, length us, event | category | flops | bytes accessed | tf_op | source)
XLA Modules:
  0.0 442.8 jit_solution(125744687563425266)
XLA Ops:
  6.5 0.1 negate_convert_fusion
  6.6 0.1 fusion.32
  6.7 0.0 copy-start.10
  6.7 5.3 %fusion.42 = (bf16[2,16,128,512]{3,2,1,0:T(8,128)(2,1)}, bf16[2,16,128,512]{3,2,1,0:T(8,128)(2,1)S(1)}) fusion(bf16[2,16,128,1024]{3,2,1,0:T(8,128)(2,1)} %param.4), kind=kLoop, calls=%fused_computation.107 | loop fusion | bytes 16777216 | tf_op jit(solution)/shard_map/slice | solution.py:94
  11.9 0.1 maximum_maximum_fusion
  12.0 6.2 %multiply_convert_fusion = bf16[16,2,128,512]{3,0,2,1:T(8,128)(2,1)S(1)} fusion(f32[128]{0:T(128)S(1)} %copy-done.10, bf16[16,2,32,1]{2,0,3,1:T(8,128)(2,1)S(1)} %bitcast.153, bf16[4,8,128,512]{3,2,1,0:T(8,128)(2,1)S(1)} %bitcast.149), kind=kOutput, calls=%fused_computation.6 | convolution fusion | flops 138412032 | bytes 8391168 | tf_op jit(solution)/shard_map/dot_general | solution.py:95
  18.2 4.4 copy.28
  22.6 6.5 %all-to-all-start.1 = ((bf16[16,2,128,512]{3,2,1,0:T(8,128)(2,1)}), bf16[16,2,128,512]{3,2,1,0:T(8,128)(2,1)}, u32[]{:S(2)}, u32[]{:S(2)}) async-start(bf16[16,2,128,512]{3,2,1,0:T(8,128)(2,1)} %copy.28), calls=%async_computation.1 | async-start | bytes 8388608 | tf_op jit(solution)/shard_map/all_to_all | solution.py:101
  29.1 0.0 copy-done.6
  29.1 0.1 dynamic-slice_bitcast_fusion
  29.2 0.1 collective-permute-start
  29.2 1.6 collective-permute-start.1
  30.8 1.4 collective-permute-start.2
  32.2 7.5 %multiply_convert_fusion.1 = bf16[16,2,128,512]{3,0,2,1:T(8,128)(2,1)} fusion(f32[128]{0:T(128)S(1)} %copy-done.10, bf16[16,2,32,1]{2,0,3,1:T(8,128)(2,1)S(1)} %bitcast.154, bf16[4,8,128,512]{3,2,1,0:T(8,128)(2,1)} %bitcast.148), kind=kOutput, calls=%fused_computation.7 | convolution fusion | flops 138412032 | bytes 8391168 | tf_op jit(solution)/shard_map/dot_general | solution.py:95
  39.8 0.0 collective-permute-done
  39.8 0.0 collective-permute-done.1
  39.8 2.7 collective-permute-done.2
  42.5 0.1 maximum_bitcast_fusion.3
  42.6 0.6 gather_fusion
  43.2 0.2 copy_bitcast_fusion
  43.4 6.5 %copy.25 = bf16[16,2,128,512]{3,2,1,0:T(8,128)(2,1)} copy(bf16[16,2,128,512]{3,0,2,1:T(8,128)(2,1)} %multiply_convert_fusion.1) | data formatting | bytes 8388608 | tf_op jit(solution)/shard_map/optimization_barrier | solution.py:99
  49.9 72.6 %all-to-all-done.1 = bf16[16,2,128,512]{3,2,1,0:T(8,128)(2,1)} async-done(((bf16[16,2,128,512]{3,2,1,0:T(8,128)(2,1)}), bf16[16,2,128,512]{3,2,1,0:T(8,128)(2,1)}, u32[]{:S(2)}, u32[]{:S(2)}) %all-to-all-start.1) | async-done | bytes 4194336 | tf_op jit(solution)/shard_map/all_to_all | solution.py:101
  122.5 5.1 %all-to-all-start = ((bf16[16,2,128,512]{3,2,1,0:T(8,128)(2,1)}), bf16[16,2,128,512]{3,2,1,0:T(8,128)(2,1)}, u32[]{:S(2)}, u32[]{:S(2)}) async-start(bf16[16,2,128,512]{3,2,1,0:T(8,128)(2,1)} %copy.25), calls=%async_computation | async-start | bytes 8388608 | tf_op jit(solution)/shard_map/all_to_all | solution.py:101
  127.6 0.0 reduce-scatter.2.cloned.1.call-start
  127.6 4.6 %copy.29 = bf16[4,4,2,128,512]{4,3,0,2,1:T(8,128)(2,1)} copy(bf16[4,4,2,128,512]{4,3,2,1,0:T(8,128)(2,1)} %bitcast.25) | data formatting | bytes 8388608 | tf_op jit(solution)/shard_map/all_to_all | solution.py:101
  132.3 87.9 %all-to-all-done = bf16[16,2,128,512]{3,2,1,0:T(8,128)(2,1)} async-done(((bf16[16,2,128,512]{3,2,1,0:T(8,128)(2,1)}), bf16[16,2,128,512]{3,2,1,0:T(8,128)(2,1)}, u32[]{:S(2)}, u32[]{:S(2)}) %all-to-all-start) | async-done | bytes 4194336 | tf_op jit(solution)/shard_map/all_to_all | solution.py:101
  220.2 2.5 copy.26
  222.7 8.1 %fusion.43 = f32[4,1024,1024]{2,1,0:T(8,128)} fusion(bf16[4,1024,512]{2,1,0:T(8,128)(2,1)S(1)} %bitcast.144), kind=kOutput, calls=%fused_computation.110 | convolution fusion | flops 4294967296 | bytes 20971520 | tf_op jit(solution)/shard_map/cat,cbt->cab/dot_general | solution.py:110
  230.8 0.0 copy-done.1
  230.8 18.5 %convolution_add_fusion = f32[4,1024,1024]{2,1,0:T(8,128)} fusion(f32[4,1024,1024]{2,1,0:T(8,128)} %fusion.43, bf16[4,1024,512]{2,1,0:T(8,128)(2,1)} %bitcast.142), kind=kOutput, calls=%fused_computation.3 | convolution fusion | flops 4299161600 | bytes 37748736 | tf_op jit(solution)/shard_map/cat,cbt->cab/dot_general | solution.py:110
  249.3 6.7 %fusion.7 = (bf16[4,512,512]{2,1,0:T(8,128)(2,1)S(1)}, bf16[4,512,512]{2,1,0:T(8,128)(2,1)S(1)}) fusion(f32[4,1024,1024]{2,1,0:T(8,128)} %convolution_add_fusion), kind=kLoop, calls=%fused_computation.19 | loop fusion | flops 4194304 | bytes 20971520 | tf_op jit(solution)/shard_map/convert.2
  256.0 2.2 pad_maximum_fusion.4
  258.2 0.0 reduce-scatter.2.cloned.1.call-update
  258.3 0.0 all-gather.2.cloned.1.call-start
  258.3 0.6 copy-done.9
  258.9 1.6 gather_fusion.1
  260.6 5.6 %select_cosine_fusion = (f32[512,512]{1,0:T(8,128)}, f32[512,512]{1,0:T(8,128)}) fusion(f32[512,512]{1,0:T(8,128)S(1)} %gather_fusion.1, pred[512]{0:T(512)(128)(4,1)S(1)} %compare_and_fusion), kind=kLoop, calls=%fused_computation.66 | loop fusion | flops 262144 | bytes 3146240 | tf_op jit(solution)/shard_map/cos | solution.py:122
  266.1 36.0 %reduce-scatter.2.cloned.1.call-done = bf16[1,1024,512]{2,1,0:T(8,128)(2,1)} async-done(((bf16[4,1024,512]{2,1,0:T(8,128)(2,1)}), bf16[1,1024,512]{2,1,0:T(8,128)(2,1)}) %reduce-scatter.2.cloned.1.call-update) | async-done | bytes 1048592 | tf_op jit(solution)/shard_map/reduce_scatter | solution.py:116
  302.1 1.5 convert_multiply_fusion
  303.7 0.1 slice_bitcast_fusion.2
  303.7 4.9 %gather_fusion.2 = f32[512]{0:T(512)S(1)} fusion(f32[512,512]{1,0:T(8,128)S(1)} %slice_bitcast_fusion.2, s32[512]{0:T(512)S(1)} %bitcast.146), kind=kCustom, calls=%fused_computation.2 | custom fusion | bytes 8192 | tf_op jit(solution)/shard_map/jit(diagonal)/gather | solution.py:27
  308.7 0.6 reduce.6
  309.9 1.8 sqrt_reduce_fusion
  311.7 0.6 reduce_max.11
  313.7 6.8 %convolution_subtract_fusion.4 = f32[1024,512]{1,0:T(8,128)S(1)} fusion(f32[512,512]{1,0:T(8,128)} %get-tuple-element.22, f32[512,512]{1,0:T(8,128)} %get-tuple-element.21, f32[1,512,512]{2,1,0:T(8,128)} %get-tuple-element.19, f32[1,512,512]{2,1,0:T(8,128)} %get-tuple-element.20, f32[1,512,512]{2,1,0:T(8,128)S(1)} %get-tuple-element.18, f32[]{:T(128)} %bitcast.32), kind=kOutput, calls=%fused_computation.46 | convolution fusion | flops 3226468352 | bytes 7340036 | tf_op jit(solution)/shard_map/eval_jaxpr/cjk,ckb->cjb/dot_general | solution.py:50
  320.5 3.6 convolution_subtract_fusion.3
  324.1 0.0 copy-start.12
  324.2 4.3 multiply_add_fusion.3
  328.5 3.8 convolution_subtract_fusion.1
  332.2 3.5 convolution_subtract_fusion
  335.8 3.6 fusion.12
  339.4 8.2 %multiply_reduce_fusion = (f32[512]{0:T(512)S(1)}, f32[1024,512]{1,0:T(8,128)S(1)}) fusion(f32[512,512]{1,0:T(8,128)S(1)} %copy-done.8, f32[512,512]{1,0:T(8,128)S(1)} %copy-done.7, f32[1024,512]{1,0:T(8,128)S(1)} %convolution_subtract_fusion, f32[1024,512]{1,0:T(8,128)S(1)} %fusion.12, f32[]{:T(128)} %bitcast.47, f32[]{:T(128)} %bitcast.46, f32[]{:T(128)} %bitcast.45, ...), kind=kOutput, calls=%fused_computation.30 | convolution fusion | flops 3245866496 | bytes 19925044 | tf_op jit(solution)/shard_map/eval_jaxpr/cjk,ckb->cjb/dot_general | solution.py:50
  347.6 1.3 divide_convert_fusion
  348.9 0.0 all-gather.2.cloned.1.call-update
  348.9 34.6 %all-gather.2.cloned.1.call-done = bf16[4,2,512,512]{3,2,0,1:T(8,128)(2,1)} async-done(((bf16[1,2,512,512]{3,2,0,1:T(8,128)(2,1)}), bf16[4,2,512,512]{3,2,0,1:T(8,128)(2,1)}) %all-gather.2.cloned.1.call-update) | async-done | bytes 4194320 | tf_op jit(solution)/shard_map/all_gather | solution.py:125
  383.5 2.7 slice_bitcast_fusion
  386.2 0.8 copy-done.3
  387.0 0.1 fusion.38
  387.1 4.1 maximum_bitcast_fusion.1
  391.2 0.4 copy-done.2
  391.6 10.2 %fusion.8 = bf16[4,512,2,512]{3,1,2,0:T(8,128)(2,1)} fusion(bf16[4,1024,512,1]{2,1,3,0:T(8,128)(2,1)S(1)} %bitcast.145, bf16[4,1024,1,512]{3,1,2,0:T(8,128)(2,1)} %get-tuple-element.16, bf16[4,1024,1,512]{3,1,2,0:T(8,128)(2,1)} %get-tuple-element.15), kind=kOutput, calls=%fused_computation.24 | convolution fusion | flops 4313841664 | bytes 16777216 | tf_op jit(solution)/shard_map/cat,cakb->ctkb/dot_general | solution.py:138
  401.8 10.1 %fusion.9 = bf16[4,512,2,512]{3,1,2,0:T(8,128)(2,1)} fusion(bf16[4,1024,512,1]{2,1,3,0:T(8,128)(2,1)S(1)} %bitcast.143, bf16[4,1024,1,512]{3,1,2,0:T(8,128)(2,1)} %get-tuple-element.16, bf16[4,1024,1,512]{3,1,2,0:T(8,128)(2,1)} %get-tuple-element.15), kind=kOutput, calls=%fused_computation.25 | convolution fusion | flops 4313841664 | bytes 16777216 | tf_op jit(solution)/shard_map/cat,cakb->ctkb/dot_general | solution.py:138
  411.9 7.2 %pad_maximum_fusion.1 = bf16[4,1024,2,512]{3,1,2,0:T(8,128)(2,1)} fusion(bf16[4,512,2,512]{3,1,2,0:T(8,128)(2,1)} %fusion.9, bf16[4,512,2,512]{3,1,2,0:T(8,128)(2,1)} %fusion.8), kind=kLoop, calls=%fused_computation.5 | loop fusion | flops 16777216 | bytes 16777216 | tf_op jit(solution)/shard_map/concatenate | solution.py:141
  419.1 16.4 %copy.34 = bf16[4,1024,2,512]{3,2,1,0:T(2,128)(2,1)} copy(bf16[4,1024,2,512]{3,1,2,0:T(8,128)(2,1)} %pad_maximum_fusion.1) | data formatting | bytes 16777216 | tf_op jit(solution)/shard_map/concatenate | solution.py:141
  (26 shorter events, 0.1 us)
Async XLA Ops:
  6.7 5.4 %copy-start.10 = (f32[128]{0:T(128)S(1)}, f32[128]{0:T(128)}, u32[]{:S(2)}) copy-start(f32[128]{0:T(128)} %param.5) | copy-start | bytes 1540
  22.6 6.5 %copy-start.6 = (f32[4,512,128]{2,1,0:T(8,128)S(1)}, f32[4,512,128]{2,1,0:T(8,128)}, u32[]{:S(2)}) copy-start(f32[4,512,128]{2,1,0:T(8,128)} %param.7) | copy-start | bytes 3145732
  22.6 99.9 %all-to-all-start.1 = ((bf16[16,2,128,512]{3,2,1,0:T(8,128)(2,1)}), bf16[16,2,128,512]{3,2,1,0:T(8,128)(2,1)}, u32[]{:S(2)}, u32[]{:S(2)}) async-start(bf16[16,2,128,512]{3,2,1,0:T(8,128)(2,1)} %copy.28), calls=%async_computation.1 | async-start | bytes 8388608 | tf_op jit(solution)/shard_map/all_to_all | solution.py:101
  29.2 10.6 %collective-permute-start = (f32[1,512,128]{2,1,0:T(8,128)S(1)}, f32[1,512,128]{2,1,0:T(8,128)S(1)}, u32[]{:S(2)}, u32[]{:S(2)}) collective-permute-start(f32[1,512,128]{2,1,0:T(8,128)S(1)} %get-tuple-element.24), channel_id=1, source_target_pairs={{0,1},{1,2},{2,3},{3,0},{4,5},{5,6},{6,7},{7,4},{8,9},{9,10},{10,1... | collective-permute-start | bytes 786440 | tf_op jit(solution)/shard_map/ppermute | solution.py:71
  29.2 10.6 %collective-permute-start.1 = (f32[1,512,128]{2,1,0:T(8,128)S(1)}, f32[1,512,128]{2,1,0:T(8,128)S(1)}, u32[]{:S(2)}, u32[]{:S(2)}) collective-permute-start(f32[1,512,128]{2,1,0:T(8,128)S(1)} %get-tuple-element.26), channel_id=1, source_target_pairs={{0,2},{1,3},{2,0},{3,1},{4,6},{5,7},{6,4},{7,5},{8,10},{9,11},{10,... | collective-permute-start | bytes 786440 | tf_op jit(solution)/shard_map/ppermute | solution.py:71
  30.8 11.7 %collective-permute-start.2 = (f32[1,512,128]{2,1,0:T(8,128)S(1)}, f32[1,512,128]{2,1,0:T(8,128)S(1)}, u32[]{:S(2)}, u32[]{:S(2)}) collective-permute-start(f32[1,512,128]{2,1,0:T(8,128)S(1)} %get-tuple-element.25), channel_id=1, source_target_pairs={{0,3},{1,0},{2,1},{3,2},{4,7},{5,4},{6,5},{7,6},{8,11},{9,8},{10,9... | collective-permute-start | bytes 786440 | tf_op jit(solution)/shard_map/ppermute | solution.py:71
  122.5 97.7 %all-to-all-start = ((bf16[16,2,128,512]{3,2,1,0:T(8,128)(2,1)}), bf16[16,2,128,512]{3,2,1,0:T(8,128)(2,1)}, u32[]{:S(2)}, u32[]{:S(2)}) async-start(bf16[16,2,128,512]{3,2,1,0:T(8,128)(2,1)} %copy.25), calls=%async_computation | async-start | bytes 8388608 | tf_op jit(solution)/shard_map/all_to_all | solution.py:101
  127.6 174.6 %reduce-scatter.2.cloned.1.call-start = ((), (), s32[]{:S(2)}) async-start(), calls=%async_computation.3 | async-start | bytes 5242880 | tf_op jit(solution)/shard_map/reduce_scatter | solution.py:116
  222.6 8.1 %copy-start.1 = (bf16[4,4,2,128,512]{4,3,0,2,1:T(8,128)(2,1)}, bf16[4,4,2,128,512]{4,3,0,2,1:T(8,128)(2,1)S(1)}, u32[]{:S(2)}) copy-start(bf16[4,4,2,128,512]{4,3,0,2,1:T(8,128)(2,1)S(1)} %copy.26) | copy-start | bytes 12582916
  258.2 0.7 copy-start.9
  258.3 125.3 %all-gather.2.cloned.1.call-start = ((), (), s32[]{:S(2)}) async-start(), calls=%async_computation.4 | async-start | bytes 5242880 | tf_op jit(solution)/shard_map/all_gather | solution.py:125
  313.6 6.8 %copy-start.4 = (f32[1,512,512]{2,1,0:T(8,128)S(1)}, f32[1,512,512]{2,1,0:T(8,128)}, u32[]{:S(2)}) copy-start(f32[1,512,512]{2,1,0:T(8,128)} %get-tuple-element.19) | copy-start | bytes 3145732
  313.6 6.8 %copy-start.5 = (f32[1,512,512]{2,1,0:T(8,128)S(1)}, f32[1,512,512]{2,1,0:T(8,128)}, u32[]{:S(2)}) copy-start(f32[1,512,512]{2,1,0:T(8,128)} %get-tuple-element.20) | copy-start | bytes 3145732
  313.7 6.8 %copy-start.7 = (f32[512,512]{1,0:T(8,128)S(1)}, f32[512,512]{1,0:T(8,128)}, u32[]{:S(2)}) copy-start(f32[512,512]{1,0:T(8,128)} %get-tuple-element.21) | copy-start | bytes 3145732
  313.7 6.8 %copy-start.8 = (f32[512,512]{1,0:T(8,128)S(1)}, f32[512,512]{1,0:T(8,128)}, u32[]{:S(2)}) copy-start(f32[512,512]{1,0:T(8,128)} %get-tuple-element.22) | copy-start | bytes 3145732
  320.5 3.7 copy-start.11
  324.1 4.3 copy-start.12
  383.5 3.4 copy-start.3
  387.1 4.5 %copy-start.2 = (bf16[4,4,2,128,512]{4,3,0,2,1:T(8,128)(2,1)S(1)}, bf16[4,4,2,128,512]{4,3,0,2,1:T(8,128)(2,1)}, u32[]{:S(2)}) copy-start(bf16[4,4,2,128,512]{4,3,0,2,1:T(8,128)(2,1)} %copy-done.1) | copy-start | bytes 12582916
  391.6 10.2 %copy-start = (bf16[4,4,2,128,512]{4,3,0,2,1:T(8,128)(2,1)S(1)}, bf16[4,4,2,128,512]{4,3,0,2,1:T(8,128)(2,1)}, u32[]{:S(2)}) copy-start(bf16[4,4,2,128,512]{4,3,0,2,1:T(8,128)(2,1)} %copy.29) | copy-start | bytes 12582916
Sparse Core Ops, SparseCore 0:
  258.4 43.7 reduce-scatter.1
  349.0 34.4 all-gather.1
